TPU v7x, 512 devices: a whole 4x4x16 slice. The times are simulated.
512 devices in a mesh: ctx: 64 (over z, y), exp: 8 (over x, core).
Axes of the slice: x: 4, y: 4, z: 16, core: 2. Of those that a mesh axis runs over, the one named last changes fastest.
Arguments:
- queries: bfloat16 [8, 8192, 2048], P('exp', 'ctx'), may hold values from -64 to 64
- rotated_key_rows: bfloat16 [8, 8192, 256], P('exp', 'ctx'), may hold values from -7 to 7
- value_row_array: bfloat16 [8, 8192, 256], P('exp', 'ctx'), may hold values from -6 to 6
- residual: bfloat16 [8, 8192, 2048], P('exp', 'ctx'), may hold values from -40 to 40
- norm_gain: float32 [2048], replicated, may hold values from 0.1 to 1.9
- expert_ids: int32 [8, 8192, 1], P('exp', 'ctx'), may hold values from 0 to 127; in each aligned block of 128 rows (0 to 127, 128 to 255, ..., all dimensions but the last counted through in order) at most 2 rows name the same one
- gate_values: float32 [8, 8192, 1], P('exp', 'ctx'), may hold values from 0.25 to 1
- w_gate_up: bfloat16 [64, 8, 2, 192, 2048], P('ctx', 'exp'), may hold values from -0.125 to 0.125
- w_down: bfloat16 [64, 8, 192, 2048], P('ctx', 'exp'), may hold values from -0.21875 to 0.21875
Outputs:
- layer_out: bfloat16 [8, 8192, 2048], P('exp', 'ctx')
Inputs may be any that keep to these rules, and one draw needn't show every extreme that they name: `expert_ids`: among the rows of one device (aligned blocks of 128 tokens along the second dimension) no expert is named more than 2 times, a bound that some block reaches.
All inputs are finite; a program needn't handle non-finite values.
Results may differ from a plain program's by a relative error of at most 0.013.
Values may be sent and summed in bfloat16 or wider, within the bound.
No kernel may reach another device: no remote copies, remote signals or barrier semaphores. Data moves between devices by JAX's collectives and lax.ppermute only.
A program may use at most 64 MiB of HBM per device.

v0:
```python
import math

import jax
import jax.numpy as jnp
from jax import lax
from jax.sharding import PartitionSpec as P

D = 2048
QUERY_HEADS = 16
KEY_VALUE_HEADS = 2
HEAD_SIZE = 128
TOP = 1


NEGATIVE_FILL = -1e30


def passed_along(value, axis, steps):
    count = lax.axis_size(axis)
    leading, last = (max(0, -steps), min(count, count - steps))
    return lax.ppermute(value, axis, [(source, source + steps) for source in range(leading, last)])


def attend_piece(soft_state, query_head_rows, key_value_block, allowed):
    row_peak, row_total, weighted_sum = soft_state
    block_key_rows = key_value_block[0].reshape(-1, KEY_VALUE_HEADS, HEAD_SIZE)
    block_value_rows = key_value_block[1].reshape(-1, KEY_VALUE_HEADS, HEAD_SIZE)
    scores = jnp.einsum(
        "qhgd,khd->hgqk", query_head_rows, block_key_rows, preferred_element_type=jnp.float32
    ) / math.sqrt(HEAD_SIZE)
    if allowed is not None:
        scores = jnp.where(allowed, scores, NEGATIVE_FILL)
    new_peak = jnp.maximum(row_peak, jnp.max(scores, axis=-1))
    expo_vals = jnp.exp(scores - new_peak[..., None])
    factor = jnp.exp(row_peak - new_peak)
    row_total = row_total * factor + jnp.sum(expo_vals, axis=-1)
    weights = expo_vals.astype(jnp.bfloat16)
    weighted_sum = weighted_sum * factor[..., None] + jnp.einsum(
        "hgqk,khd->hgqd", weights, block_value_rows, preferred_element_type=jnp.float32
    )
    return (new_peak, row_total, weighted_sum)


def on_device(
    queries,
    rotated_key_rows,
    value_row_array,
    residual,
    norm_gain,
    expert_ids,
    gate_values,
    w_gate_up,
    w_down,
):
    ctx_count = lax.axis_size("ctx")
    exp_count = lax.axis_size("exp")
    token_rows = queries.shape[1]
    queries_per_key_head = QUERY_HEADS // KEY_VALUE_HEADS
    query_head_rows = queries[0].reshape(
        token_rows, KEY_VALUE_HEADS, queries_per_key_head, HEAD_SIZE
    )
    prompt_devs = ctx_count // 2
    ctx_index = lax.axis_index("ctx")
    in_prompt = ctx_index // 2
    own_block = jnp.stack([rotated_key_rows[0], value_row_array[0]])
    diagonal = jnp.arange(token_rows)[:, None] >= jnp.arange(token_rows)[None, :]
    start_state = (
        jnp.full((KEY_VALUE_HEADS, queries_per_key_head, token_rows), NEGATIVE_FILL, jnp.float32),
        jnp.zeros((KEY_VALUE_HEADS, queries_per_key_head, token_rows), jnp.float32),
        jnp.zeros((KEY_VALUE_HEADS, queries_per_key_head, token_rows, HEAD_SIZE), jnp.float32),
    )
    soft_state = attend_piece(start_state, query_head_rows, own_block, diagonal)

    def carry_step(step_index, carried):
        current_state, moving = carried
        moving = passed_along(moving, "ctx", 2)
        current_state = lax.cond(
            step_index <= in_prompt,
            lambda state_in: attend_piece(state_in, query_head_rows, moving, None),
            lambda state_in: state_in,
            current_state,
        )
        return (current_state, moving)

    soft_state, _ = lax.fori_loop(1, prompt_devs, carry_step, (soft_state, own_block))
    row_peak, row_total, weighted_sum = soft_state
    attended_rows = weighted_sum / row_total[..., None]
    attended_rows = jnp.transpose(attended_rows, (2, 0, 1, 3)).reshape(
        token_rows, QUERY_HEADS * HEAD_SIZE
    )
    mid_rows = (residual[0].astype(jnp.float32) + attended_rows).astype(jnp.bfloat16)
    mid_wide = mid_rows.astype(jnp.float32)
    inverse = lax.rsqrt(jnp.mean(mid_wide * mid_wide, axis=-1, keepdims=True) + 1e-06)
    normed = (mid_wide * inverse * norm_gain).astype(jnp.bfloat16)
    per_group = ctx_count // 4
    expert_count = per_group * exp_count
    slot_depth = max(2, 2 * token_rows * TOP // expert_count)
    assign_count = token_rows * TOP
    routed = expert_ids[0].reshape(assign_count)
    onehot_table = (routed[:, None] == jnp.arange(expert_count)[None, :]).astype(jnp.float32)
    earlier_blocks = (jnp.arange(assign_count)[:, None] > jnp.arange(assign_count)[None, :]).astype(
        jnp.float32
    )
    before = jnp.dot(
        earlier_blocks,
        onehot_table,
        precision=lax.Precision.HIGHEST,
        preferred_element_type=jnp.float32,
    )
    rank_in = jnp.sum(before * onehot_table, axis=1).astype(jnp.int32)
    slot_index = (routed % per_group * exp_count + routed // per_group) * slot_depth + rank_in
    slot_count = expert_count * slot_depth
    placement = (jnp.arange(slot_count)[:, None] == slot_index[None, :]).astype(jnp.bfloat16)
    normed_assign = jnp.repeat(normed, TOP, axis=0)
    outgoing = jnp.dot(placement, normed_assign, preferred_element_type=jnp.float32).astype(
        jnp.bfloat16
    )
    outgoing = outgoing.reshape(per_group, exp_count, slot_depth, D)
    incoming = lax.all_to_all(outgoing, "exp", split_axis=1, concat_axis=1, tiled=True)
    slot_width = exp_count * slot_depth
    by_expert = incoming.reshape(per_group, slot_width, D)
    gate_up = w_gate_up[0, 0]
    down_rows = w_down[0, 0]
    copies = jnp.broadcast_to(by_expert[:, None], (per_group, 4, slot_width, D)).reshape(
        ctx_count, slot_width, D
    )
    arrived = lax.all_to_all(copies, "ctx", split_axis=0, concat_axis=0, tiled=True)
    lead_shape = arrived.shape[:-1]
    flat_rows = arrived.reshape(-1, D)
    projected = lax.dot_general(
        gate_up, flat_rows, (((2,), (1,)), ((), ())), preferred_element_type=jnp.float32
    )
    hidden = (jax.nn.silu(projected[0]) * projected[1]).astype(jnp.bfloat16)
    part_out = lax.dot_general(
        hidden, down_rows, (((0,), (0,)), ((), ())), preferred_element_type=jnp.float32
    )
    partial_value = part_out.astype(jnp.bfloat16).reshape(lead_shape + (D,))
    returned = lax.all_to_all(partial_value, "ctx", split_axis=0, concat_axis=0, tiled=True)
    returned = returned.reshape(per_group, 4, slot_width, D)
    summed = (
        returned[:, 0].astype(jnp.float32)
        + returned[:, 1].astype(jnp.float32)
        + returned[:, 2].astype(jnp.float32)
        + returned[:, 3].astype(jnp.float32)
    ).astype(jnp.bfloat16)
    delivered = lax.all_to_all(
        summed.reshape(per_group, exp_count, slot_depth, D),
        "exp",
        split_axis=1,
        concat_axis=1,
        tiled=True,
    )
    expert_out = lax.dot_general(
        placement,
        delivered.reshape(slot_count, D),
        (((0,), (0,)), ((), ())),
        preferred_element_type=jnp.float32,
    )
    gated = expert_out.reshape(token_rows, TOP, D) * gate_values[0][:, :, None]
    layer_out = (mid_wide + jnp.sum(gated, axis=1)).astype(jnp.bfloat16)
    return layer_out[None]


def solution(mesh):
    return jax.shard_map(
        on_device,
        mesh=mesh,
        in_specs=(
            P("exp", "ctx", None),
            P("exp", "ctx", None),
            P("exp", "ctx", None),
            P("exp", "ctx", None),
            P(),
            P("exp", "ctx", None),
            P("exp", "ctx", None),
            P("ctx", "exp", None, None, None),
            P("ctx", "exp", None, None),
        ),
        out_specs=P("exp", "ctx", None),
        check_vma=False,
    )
```

profile of v0, /device:TPU:1, one launch (start us, length us, event | category | flops | bytes accessed | tf_op | source)
XLA Modules:
  0.0 838.3 jit_solution(11995129742699127945)
XLA Ops:
  12.0 282.2 %while.19 = (s32[]{:T(128)}, f32[2,8,128]{2,1,0:T(8,128)S(1)}, f32[2,8,128]{2,1,0:T(8,128)S(1)}, f32[2,8,128,128]{3,2,1,0:T(8,128)S(1)}, bf16[2,128,256]{1,2,0:T...) while((s32[]{:T(128)}, f32[2,8,128]{2,1,0:T(8,128)S(1)}, ...), condition=%wide.region_7.8_spmd, body=%wide.region_2.7_spmd.sunk | while | flops 136318976 | bytes 7078123 | solution.py:85
  12.0 5.6 collective-permute-start
  19.6 6.6 collective-permute-start
  28.2 5.3 collective-permute-start
  33.5 1.9 collective-permute-done
  35.4 7.0 collective-permute-start
  42.4 1.9 collective-permute-done
  44.3 6.2 collective-permute-start
  52.5 6.2 collective-permute-start
  58.7 1.9 collective-permute-done
  60.6 6.2 collective-permute-start
  66.8 1.9 collective-permute-done
  68.8 6.2 collective-permute-start
  75.0 2.6 collective-permute-done
  77.6 6.5 collective-permute-start
  84.1 2.8 collective-permute-done
  86.9 5.9 collective-permute-start
  92.9 1.9 collective-permute-done
  94.8 6.5 collective-permute-start
  101.4 1.9 collective-permute-done
  103.3 6.2 collective-permute-start
  111.4 6.2 collective-permute-start
  119.6 6.9 collective-permute-start
  126.5 1.9 collective-permute-done
  128.5 9.2 %collective-permute-start = (bf16[2,128,256]{1,2,0:T(8,128)(2,1)S(1)}, bf16[2,128,256]{1,2,0:T(8,128)(2,1)S(1)}, u32[]{:S(2)}, u32[]{:S(2)}) collective-permute-start(bf16[2,128,256]{1,2,0:T(8,128)(2,1)S(1)} %get-tuple-element.283), channel_id=1, source_target_pairs={{0,16},{8,24},{16,32},{24,40},{32,48},{40,56},{48,64},{56,72},{64,... | collective-permute-start | bytes 393224 | tf_op jit(solution)/shard_map/while/body/eval_jaxpr/ppermute | solution.py:21
  137.7 1.9 collective-permute-done
  139.6 8.3 collective-permute-start
  148.0 1.9 collective-permute-done
  149.9 6.2 collective-permute-start
  158.1 7.6 collective-permute-start
  165.7 1.9 collective-permute-done
  167.7 7.4 collective-permute-start
  177.0 7.4 collective-permute-start
  184.4 2.6 collective-permute-done
  187.1 7.8 collective-permute-start
  194.9 2.8 collective-permute-done
  197.7 7.8 collective-permute-start
  205.6 1.9 collective-permute-done
  207.5 7.2 collective-permute-start
  214.7 1.9 collective-permute-done
  216.7 7.2 collective-permute-start
  223.9 1.9 collective-permute-done
  225.8 7.8 collective-permute-start
  235.6 6.8 collective-permute-start
  242.5 1.9 collective-permute-done
  244.4 7.7 collective-permute-start
  252.2 1.9 collective-permute-done
  254.1 7.7 collective-permute-start
  263.8 7.4 collective-permute-start
  273.2 7.6 collective-permute-start
  280.8 3.0 collective-permute-done
  283.8 8.0 collective-permute-start
  291.8 2.4 collective-permute-done
  298.4 2.5 reshape.129
  301.0 2.1 copy.79
  303.0 51.8 %all_to_all.20 = bf16[16,8,2,2048]{3,2,0,1:T(2,128)(2,1)S(1)} all-to-all(bf16[16,8,2,2048]{3,2,0,1:T(2,128)(2,1)S(1)} %copy.79), channel_id=1, replica_groups=mesh['ctx'=64,'exp'=8] {'exp'}, dimensions={1} | all-to-all | bytes 2097152 | tf_op jit(solution)/shard_map/all_to_all | solution.py:119
  356.3 246.7 %all_to_all.21 = bf16[64,16,2048]{2,1,0:T(8,128)(2,1)S(1)} all-to-all(bf16[64,16,2048]{2,1,0:T(8,128)(2,1)S(1)} %bitcast.81), channel_id=1, replica_groups=mesh['ctx'=64,'exp'=8] {'ctx'}, dimensions={0} | all-to-all | bytes 8388608 | tf_op jit(solution)/shard_map/all_to_all | solution.py:127
  606.3 195.1 %all_to_all.22 = bf16[64,16,2048]{2,1,0:T(8,128)(2,1)S(1)} all-to-all(bf16[64,16,2048]{2,1,0:T(8,128)(2,1)S(1)} %bitcast.89), channel_id=1, replica_groups=mesh['ctx'=64,'exp'=8] {'ctx'}, dimensions={0} | all-to-all | bytes 8388608 | tf_op jit(solution)/shard_map/all_to_all | solution.py:138
  802.7 2.1 copy.83
  804.8 10.6 %all-to-all-start.3 = ((bf16[16,8,2,2048]{3,2,0,1:T(2,128)(2,1)}), bf16[16,8,2,2048]{3,2,0,1:T(2,128)(2,1)}, u32[]{:S(2)}, u32[]{:S(2)}) async-start(bf16[16,8,2,2048]{3,2,0,1:T(2,128)(2,1)} %copy.83), calls=%async_computation.3 | async-start | bytes 2097152 | tf_op jit(solution)/shard_map/all_to_all | solution.py:146
  816.5 14.0 %all-to-all-done.3 = bf16[16,8,2,2048]{3,2,0,1:T(2,128)(2,1)} async-done(((bf16[16,8,2,2048]{3,2,0,1:T(2,128)(2,1)}), bf16[16,8,2,2048]{3,2,0,1:T(2,128)(2,1)}, u32[]{:S(2)}, u32[]{:S(2)}) %all-to-all-start.3) | async-done | bytes 1048608 | tf_op jit(solution)/shard_map/all_to_all | solution.py:146
  830.5 3.2 copy.84
  833.7 2.3 reshape.134
  835.9 2.4 fusion.7
  (121 shorter events, 42.7 us)
Async XLA Ops:
  0.0 603.0 %copy-start = (bf16[1,1,2,192,2048]{4,3,2,1,0:T(8,128)(2,1)S(1)}, bf16[1,1,2,192,2048]{4,3,2,1,0:T(8,128)(2,1)}, u32[]{:S(2)}) copy-start(bf16[1,1,2,192,2048]{4,3,2,1,0:T(8,128)(2,1)} %param.20) | copy-start | bytes 4718596
  7.2 1.8 copy-start.2
  7.8 1.0 copy-start.1
  12.0 7.6 collective-permute-start
  19.6 8.5 %collective-permute-start = (bf16[2,128,256]{1,2,0:T(8,128)(2,1)S(1)}, bf16[2,128,256]{1,2,0:T(8,128)(2,1)S(1)}, u32[]{:S(2)}, u32[]{:S(2)}) collective-permute-start(bf16[2,128,256]{1,2,0:T(8,128)(2,1)S(1)} %get-tuple-element.283), channel_id=1, source_target_pairs={{0,16},{8,24},{16,32},{24,40},{32,48},{40,56},{48,64},{56,72},{64,... | collective-permute-start | bytes 393224 | tf_op jit(solution)/shard_map/while/body/eval_jaxpr/ppermute | solution.py:21
  28.2 7.2 collective-permute-start
  35.4 8.9 %collective-permute-start = (bf16[2,128,256]{1,2,0:T(8,128)(2,1)S(1)}, bf16[2,128,256]{1,2,0:T(8,128)(2,1)S(1)}, u32[]{:S(2)}, u32[]{:S(2)}) collective-permute-start(bf16[2,128,256]{1,2,0:T(8,128)(2,1)S(1)} %get-tuple-element.283), channel_id=1, source_target_pairs={{0,16},{8,24},{16,32},{24,40},{32,48},{40,56},{48,64},{56,72},{64,... | collective-permute-start | bytes 393224 | tf_op jit(solution)/shard_map/while/body/eval_jaxpr/ppermute | solution.py:21
  44.3 8.1 collective-permute-start
  52.5 8.1 collective-permute-start
  60.6 8.1 collective-permute-start
  68.8 8.8 %collective-permute-start = (bf16[2,128,256]{1,2,0:T(8,128)(2,1)S(1)}, bf16[2,128,256]{1,2,0:T(8,128)(2,1)S(1)}, u32[]{:S(2)}, u32[]{:S(2)}) collective-permute-start(bf16[2,128,256]{1,2,0:T(8,128)(2,1)S(1)} %get-tuple-element.283), channel_id=1, source_target_pairs={{0,16},{8,24},{16,32},{24,40},{32,48},{40,56},{48,64},{56,72},{64,... | collective-permute-start | bytes 393224 | tf_op jit(solution)/shard_map/while/body/eval_jaxpr/ppermute | solution.py:21
  77.6 9.3 %collective-permute-start = (bf16[2,128,256]{1,2,0:T(8,128)(2,1)S(1)}, bf16[2,128,256]{1,2,0:T(8,128)(2,1)S(1)}, u32[]{:S(2)}, u32[]{:S(2)}) collective-permute-start(bf16[2,128,256]{1,2,0:T(8,128)(2,1)S(1)} %get-tuple-element.283), channel_id=1, source_target_pairs={{0,16},{8,24},{16,32},{24,40},{32,48},{40,56},{48,64},{56,72},{64,... | collective-permute-start | bytes 393224 | tf_op jit(solution)/shard_map/while/body/eval_jaxpr/ppermute | solution.py:21
  86.9 7.9 collective-permute-start
  94.8 8.4 %collective-permute-start = (bf16[2,128,256]{1,2,0:T(8,128)(2,1)S(1)}, bf16[2,128,256]{1,2,0:T(8,128)(2,1)S(1)}, u32[]{:S(2)}, u32[]{:S(2)}) collective-permute-start(bf16[2,128,256]{1,2,0:T(8,128)(2,1)S(1)} %get-tuple-element.283), channel_id=1, source_target_pairs={{0,16},{8,24},{16,32},{24,40},{32,48},{40,56},{48,64},{56,72},{64,... | collective-permute-start | bytes 393224 | tf_op jit(solution)/shard_map/while/body/eval_jaxpr/ppermute | solution.py:21
  103.3 8.1 collective-permute-start
  111.4 8.1 collective-permute-start
  119.6 8.9 %collective-permute-start = (bf16[2,128,256]{1,2,0:T(8,128)(2,1)S(1)}, bf16[2,128,256]{1,2,0:T(8,128)(2,1)S(1)}, u32[]{:S(2)}, u32[]{:S(2)}) collective-permute-start(bf16[2,128,256]{1,2,0:T(8,128)(2,1)S(1)} %get-tuple-element.283), channel_id=1, source_target_pairs={{0,16},{8,24},{16,32},{24,40},{32,48},{40,56},{48,64},{56,72},{64,... | collective-permute-start | bytes 393224 | tf_op jit(solution)/shard_map/while/body/eval_jaxpr/ppermute | solution.py:21
  128.5 11.1 %collective-permute-start = (bf16[2,128,256]{1,2,0:T(8,128)(2,1)S(1)}, bf16[2,128,256]{1,2,0:T(8,128)(2,1)S(1)}, u32[]{:S(2)}, u32[]{:S(2)}) collective-permute-start(bf16[2,128,256]{1,2,0:T(8,128)(2,1)S(1)} %get-tuple-element.283), channel_id=1, source_target_pairs={{0,16},{8,24},{16,32},{24,40},{32,48},{40,56},{48,64},{56,72},{64,... | collective-permute-start | bytes 393224 | tf_op jit(solution)/shard_map/while/body/eval_jaxpr/ppermute | solution.py:21
  139.6 10.3 %collective-permute-start = (bf16[2,128,256]{1,2,0:T(8,128)(2,1)S(1)}, bf16[2,128,256]{1,2,0:T(8,128)(2,1)S(1)}, u32[]{:S(2)}, u32[]{:S(2)}) collective-permute-start(bf16[2,128,256]{1,2,0:T(8,128)(2,1)S(1)} %get-tuple-element.283), channel_id=1, source_target_pairs={{0,16},{8,24},{16,32},{24,40},{32,48},{40,56},{48,64},{56,72},{64,... | collective-permute-start | bytes 393224 | tf_op jit(solution)/shard_map/while/body/eval_jaxpr/ppermute | solution.py:21
  149.9 8.1 collective-permute-start
  158.1 9.6 %collective-permute-start = (bf16[2,128,256]{1,2,0:T(8,128)(2,1)S(1)}, bf16[2,128,256]{1,2,0:T(8,128)(2,1)S(1)}, u32[]{:S(2)}, u32[]{:S(2)}) collective-permute-start(bf16[2,128,256]{1,2,0:T(8,128)(2,1)S(1)} %get-tuple-element.283), channel_id=1, source_target_pairs={{0,16},{8,24},{16,32},{24,40},{32,48},{40,56},{48,64},{56,72},{64,... | collective-permute-start | bytes 393224 | tf_op jit(solution)/shard_map/while/body/eval_jaxpr/ppermute | solution.py:21
  167.7 9.3 %collective-permute-start = (bf16[2,128,256]{1,2,0:T(8,128)(2,1)S(1)}, bf16[2,128,256]{1,2,0:T(8,128)(2,1)S(1)}, u32[]{:S(2)}, u32[]{:S(2)}) collective-permute-start(bf16[2,128,256]{1,2,0:T(8,128)(2,1)S(1)} %get-tuple-element.283), channel_id=1, source_target_pairs={{0,16},{8,24},{16,32},{24,40},{32,48},{40,56},{48,64},{56,72},{64,... | collective-permute-start | bytes 393224 | tf_op jit(solution)/shard_map/while/body/eval_jaxpr/ppermute | solution.py:21
  177.0 10.0 %collective-permute-start = (bf16[2,128,256]{1,2,0:T(8,128)(2,1)S(1)}, bf16[2,128,256]{1,2,0:T(8,128)(2,1)S(1)}, u32[]{:S(2)}, u32[]{:S(2)}) collective-permute-start(bf16[2,128,256]{1,2,0:T(8,128)(2,1)S(1)} %get-tuple-element.283), channel_id=1, source_target_pairs={{0,16},{8,24},{16,32},{24,40},{32,48},{40,56},{48,64},{56,72},{64,... | collective-permute-start | bytes 393224 | tf_op jit(solution)/shard_map/while/body/eval_jaxpr/ppermute | solution.py:21
  187.1 10.7 %collective-permute-start = (bf16[2,128,256]{1,2,0:T(8,128)(2,1)S(1)}, bf16[2,128,256]{1,2,0:T(8,128)(2,1)S(1)}, u32[]{:S(2)}, u32[]{:S(2)}) collective-permute-start(bf16[2,128,256]{1,2,0:T(8,128)(2,1)S(1)} %get-tuple-element.283), channel_id=1, source_target_pairs={{0,16},{8,24},{16,32},{24,40},{32,48},{40,56},{48,64},{56,72},{64,... | collective-permute-start | bytes 393224 | tf_op jit(solution)/shard_map/while/body/eval_jaxpr/ppermute | solution.py:21
  197.7 9.8 %collective-permute-start = (bf16[2,128,256]{1,2,0:T(8,128)(2,1)S(1)}, bf16[2,128,256]{1,2,0:T(8,128)(2,1)S(1)}, u32[]{:S(2)}, u32[]{:S(2)}) collective-permute-start(bf16[2,128,256]{1,2,0:T(8,128)(2,1)S(1)} %get-tuple-element.283), channel_id=1, source_target_pairs={{0,16},{8,24},{16,32},{24,40},{32,48},{40,56},{48,64},{56,72},{64,... | collective-permute-start | bytes 393224 | tf_op jit(solution)/shard_map/while/body/eval_jaxpr/ppermute | solution.py:21
  207.5 9.1 %collective-permute-start = (bf16[2,128,256]{1,2,0:T(8,128)(2,1)S(1)}, bf16[2,128,256]{1,2,0:T(8,128)(2,1)S(1)}, u32[]{:S(2)}, u32[]{:S(2)}) collective-permute-start(bf16[2,128,256]{1,2,0:T(8,128)(2,1)S(1)} %get-tuple-element.283), channel_id=1, source_target_pairs={{0,16},{8,24},{16,32},{24,40},{32,48},{40,56},{48,64},{56,72},{64,... | collective-permute-start | bytes 393224 | tf_op jit(solution)/shard_map/while/body/eval_jaxpr/ppermute | solution.py:21
  216.7 9.2 %collective-permute-start = (bf16[2,128,256]{1,2,0:T(8,128)(2,1)S(1)}, bf16[2,128,256]{1,2,0:T(8,128)(2,1)S(1)}, u32[]{:S(2)}, u32[]{:S(2)}) collective-permute-start(bf16[2,128,256]{1,2,0:T(8,128)(2,1)S(1)} %get-tuple-element.283), channel_id=1, source_target_pairs={{0,16},{8,24},{16,32},{24,40},{32,48},{40,56},{48,64},{56,72},{64,... | collective-permute-start | bytes 393224 | tf_op jit(solution)/shard_map/while/body/eval_jaxpr/ppermute | solution.py:21
  225.8 9.8 %collective-permute-start = (bf16[2,128,256]{1,2,0:T(8,128)(2,1)S(1)}, bf16[2,128,256]{1,2,0:T(8,128)(2,1)S(1)}, u32[]{:S(2)}, u32[]{:S(2)}) collective-permute-start(bf16[2,128,256]{1,2,0:T(8,128)(2,1)S(1)} %get-tuple-element.283), channel_id=1, source_target_pairs={{0,16},{8,24},{16,32},{24,40},{32,48},{40,56},{48,64},{56,72},{64,... | collective-permute-start | bytes 393224 | tf_op jit(solution)/shard_map/while/body/eval_jaxpr/ppermute | solution.py:21
  235.6 8.8 %collective-permute-start = (bf16[2,128,256]{1,2,0:T(8,128)(2,1)S(1)}, bf16[2,128,256]{1,2,0:T(8,128)(2,1)S(1)}, u32[]{:S(2)}, u32[]{:S(2)}) collective-permute-start(bf16[2,128,256]{1,2,0:T(8,128)(2,1)S(1)} %get-tuple-element.283), channel_id=1, source_target_pairs={{0,16},{8,24},{16,32},{24,40},{32,48},{40,56},{48,64},{56,72},{64,... | collective-permute-start | bytes 393224 | tf_op jit(solution)/shard_map/while/body/eval_jaxpr/ppermute | solution.py:21
  244.4 9.7 %collective-permute-start = (bf16[2,128,256]{1,2,0:T(8,128)(2,1)S(1)}, bf16[2,128,256]{1,2,0:T(8,128)(2,1)S(1)}, u32[]{:S(2)}, u32[]{:S(2)}) collective-permute-start(bf16[2,128,256]{1,2,0:T(8,128)(2,1)S(1)} %get-tuple-element.283), channel_id=1, source_target_pairs={{0,16},{8,24},{16,32},{24,40},{32,48},{40,56},{48,64},{56,72},{64,... | collective-permute-start | bytes 393224 | tf_op jit(solution)/shard_map/while/body/eval_jaxpr/ppermute | solution.py:21
  254.1 9.7 %collective-permute-start = (bf16[2,128,256]{1,2,0:T(8,128)(2,1)S(1)}, bf16[2,128,256]{1,2,0:T(8,128)(2,1)S(1)}, u32[]{:S(2)}, u32[]{:S(2)}) collective-permute-start(bf16[2,128,256]{1,2,0:T(8,128)(2,1)S(1)} %get-tuple-element.283), channel_id=1, source_target_pairs={{0,16},{8,24},{16,32},{24,40},{32,48},{40,56},{48,64},{56,72},{64,... | collective-permute-start | bytes 393224 | tf_op jit(solution)/shard_map/while/body/eval_jaxpr/ppermute | solution.py:21
  263.8 9.3 %collective-permute-start = (bf16[2,128,256]{1,2,0:T(8,128)(2,1)S(1)}, bf16[2,128,256]{1,2,0:T(8,128)(2,1)S(1)}, u32[]{:S(2)}, u32[]{:S(2)}) collective-permute-start(bf16[2,128,256]{1,2,0:T(8,128)(2,1)S(1)} %get-tuple-element.283), channel_id=1, source_target_pairs={{0,16},{8,24},{16,32},{24,40},{32,48},{40,56},{48,64},{56,72},{64,... | collective-permute-start | bytes 393224 | tf_op jit(solution)/shard_map/while/body/eval_jaxpr/ppermute | solution.py:21
  273.2 10.6 %collective-permute-start = (bf16[2,128,256]{1,2,0:T(8,128)(2,1)S(1)}, bf16[2,128,256]{1,2,0:T(8,128)(2,1)S(1)}, u32[]{:S(2)}, u32[]{:S(2)}) collective-permute-start(bf16[2,128,256]{1,2,0:T(8,128)(2,1)S(1)} %get-tuple-element.283), channel_id=1, source_target_pairs={{0,16},{8,24},{16,32},{24,40},{32,48},{40,56},{48,64},{56,72},{64,... | collective-permute-start | bytes 393224 | tf_op jit(solution)/shard_map/while/body/eval_jaxpr/ppermute | solution.py:21
  283.8 10.4 %collective-permute-start = (bf16[2,128,256]{1,2,0:T(8,128)(2,1)S(1)}, bf16[2,128,256]{1,2,0:T(8,128)(2,1)S(1)}, u32[]{:S(2)}, u32[]{:S(2)}) collective-permute-start(bf16[2,128,256]{1,2,0:T(8,128)(2,1)S(1)} %get-tuple-element.283), channel_id=1, source_target_pairs={{0,16},{8,24},{16,32},{24,40},{32,48},{40,56},{48,64},{56,72},{64,... | collective-permute-start | bytes 393224 | tf_op jit(solution)/shard_map/while/body/eval_jaxpr/ppermute | solution.py:21
  294.3 2.5 copy-start.3
  294.3 2.5 copy-start.6
  294.3 2.5 copy-start.7
  603.0 1.9 copy-start.9
  804.8 25.7 %all-to-all-start.3 = ((bf16[16,8,2,2048]{3,2,0,1:T(2,128)(2,1)}), bf16[16,8,2,2048]{3,2,0,1:T(2,128)(2,1)}, u32[]{:S(2)}, u32[]{:S(2)}) async-start(bf16[16,8,2,2048]{3,2,0,1:T(2,128)(2,1)} %copy.83), calls=%async_computation.3 | async-start | bytes 2097152 | tf_op jit(solution)/shard_map/all_to_all | solution.py:146
  816.5 19.4 %copy-start.4 = (bf16[1,128,2048]{2,1,0:T(8,128)(2,1)S(1)}, bf16[1,128,2048]{2,1,0:T(8,128)(2,1)}, u32[]{:S(2)}) copy-start(bf16[1,128,2048]{2,1,0:T(8,128)(2,1)} %param.16) | copy-start | bytes 1572868
  816.5 19.4 %copy-start.5 = (f32[1,128,2048]{2,1,0:T(8,128)S(1)}, f32[1,128,2048]{2,1,0:T(8,128)}, u32[]{:S(2)}) copy-start(f32[1,128,2048]{2,1,0:T(8,128)} %reshape.127) | copy-start | bytes 3145732
  816.5 19.4 %copy-start.8 = (f32[1,128,1]{1,2,0:T(1,128)S(1)}, f32[1,128,1]{1,2,0:T(1,128)}, u32[]{:S(2)}) copy-start(f32[1,128,1]{1,2,0:T(1,128)} %param.19) | copy-start | bytes 1540
where the time goes:
time: 840 us; the launch traced here: 838 us
  blocking collectives  494 us (59%)
  starting transfers between devices  227 us (27%)
  waiting for transfers between devices  78.1 us (9%)
  local copies, waits for them, and re-layouts  23.7 us (3%)
  matrix products  10.2 us (1%)
    all_to_all x1, blocking collectives, on_device(): lax.all_to_all(copies, 'ctx', split_axis=0, concat_axis=0, tiled=True)  247 us
    ppermute x31, starting transfers between devices, passed_along(): lax.ppermute(value, axis, [(source, source + steps) for source in range(l...  217 us
    all_to_all x1, blocking collectives, on_device(): lax.all_to_all(partial_value, 'ctx', split_axis=0, concat_axis=0, tiled=T...  195 us
    ppermute x31, waiting for transfers between devices, passed_along(): lax.ppermute(value, axis, [(source, source + steps) for source in range(l...  64.2 us
    all_to_all x1, blocking collectives, on_device(): lax.all_to_all(outgoing, 'exp', split_axis=1, concat_axis=1, tiled=True)  51.8 us
  transfers between devices with their start and end apart: 32, of which 32 were waited for; matrix products, arithmetic and copies ran while one was open for 0% of the time, Pallas kernels for 0%

commit v1 on v0

v1 whole, which is shorter than its diff:
```python
import math

import jax
import jax.numpy as jnp
from jax import lax
from jax.experimental import pallas as pl
from jax.experimental.pallas import tpu as pltpu
from jax.sharding import Mesh
from jax.sharding import PartitionSpec as P

D = 2048
QUERY_HEADS = 16
KEY_VALUE_HEADS = 2
HEAD_SIZE = 128
TOP = 1
QUARTERS = 4

NEGATIVE_FILL = -1e30

CTX = ("z", "yh", "yl")
PROMPT = ("z", "yh")
QUARTER_AXES = ("yh", "yl")
ROUTE = ("z", "e")


def attend_kernel(pos_ref, q_ref, k_ref, v_ref, o_ref):
    rows_here = q_ref.shape[0]
    scores = lax.dot_general(
        q_ref[...], k_ref[...], (((1,), (1,)), ((), ())), preferred_element_type=jnp.float32
    ) / math.sqrt(HEAD_SIZE)
    query_pos = lax.broadcasted_iota(jnp.int32, scores.shape, 0) + pos_ref[0] * rows_here
    key_pos = lax.broadcasted_iota(jnp.int32, scores.shape, 1)
    scores = jnp.where(key_pos <= query_pos, scores, NEGATIVE_FILL)
    row_peak = jnp.max(scores, axis=1, keepdims=True)
    expo_vals = jnp.exp(scores - row_peak)
    row_total = jnp.sum(expo_vals, axis=1, keepdims=True)
    summed = jnp.dot(expo_vals.astype(jnp.bfloat16), v_ref[...], preferred_element_type=jnp.float32)
    o_ref[...] = summed / row_total


def attend(pos, queries, kv_all):
    rows_here = queries.shape[0]
    keys_all = kv_all.shape[0]
    per_kv = QUERY_HEADS // KEY_VALUE_HEADS
    flops = QUERY_HEADS * 4 * rows_here * keys_all * HEAD_SIZE
    grid_spec = pltpu.PrefetchScalarGridSpec(
        num_scalar_prefetch=1,
        grid=(QUERY_HEADS,),
        in_specs=[
            pl.BlockSpec((rows_here, HEAD_SIZE), lambda h, p: (0, h)),
            pl.BlockSpec((keys_all, HEAD_SIZE), lambda h, p: (0, h // per_kv)),
            pl.BlockSpec((keys_all, HEAD_SIZE), lambda h, p: (0, KEY_VALUE_HEADS + h // per_kv)),
        ],
        out_specs=pl.BlockSpec((rows_here, HEAD_SIZE), lambda h, p: (0, h)),
    )
    return pl.pallas_call(
        attend_kernel,
        out_shape=jax.ShapeDtypeStruct((rows_here, QUERY_HEADS * HEAD_SIZE), jnp.float32),
        grid_spec=grid_spec,
        cost_estimate=pl.CostEstimate(
            flops=flops,
            transcendentals=QUERY_HEADS * rows_here * keys_all,
            bytes_accessed=2 * kv_all.size * 2 + queries.size * 2 + rows_here * D * 4,
        ),
    )(pos, queries, kv_all, kv_all)


def on_device(
    queries,
    rotated_key_rows,
    value_row_array,
    residual,
    norm_gain,
    expert_ids,
    gate_values,
    w_gate_up,
    w_down,
):
    token_rows = queries.shape[1]
    route_count = lax.axis_size("z") * lax.axis_size("e")
    group_count = lax.axis_size("e")
    per_group = lax.axis_size("z")

    gate_up_all = lax.all_gather(w_gate_up[0, 0], QUARTER_AXES, axis=0, tiled=False)
    down_all = lax.all_gather(w_down[0, 0], QUARTER_AXES, axis=0, tiled=False)

    own_kv = jnp.concatenate([rotated_key_rows[0], value_row_array[0]], axis=-1)
    kv_all = lax.all_gather(own_kv, PROMPT, axis=0, tiled=True)
    pos = (lax.axis_index("z") * lax.axis_size("yh") + lax.axis_index("yh")).astype(jnp.int32)
    attended_rows = attend(pos.reshape(1), queries[0], kv_all)

    mid_rows = (residual[0].astype(jnp.float32) + attended_rows).astype(jnp.bfloat16)
    mid_wide = mid_rows.astype(jnp.float32)
    inverse = lax.rsqrt(jnp.mean(mid_wide * mid_wide, axis=-1, keepdims=True) + 1e-06)
    normed = (mid_wide * inverse * norm_gain).astype(jnp.bfloat16)

    slot_depth = max(2, 2 * token_rows * TOP // route_count)
    assign_count = token_rows * TOP
    routed = expert_ids[0].reshape(assign_count)
    onehot_table = (routed[:, None] == jnp.arange(route_count)[None, :]).astype(jnp.float32)
    earlier_blocks = (jnp.arange(assign_count)[:, None] > jnp.arange(assign_count)[None, :]).astype(
        jnp.float32
    )
    before = jnp.dot(
        earlier_blocks,
        onehot_table,
        precision=lax.Precision.HIGHEST,
        preferred_element_type=jnp.float32,
    )
    rank_in = jnp.sum(before * onehot_table, axis=1).astype(jnp.int32)
    slot_index = (routed % per_group * group_count + routed // per_group) * slot_depth + rank_in
    slot_count = route_count * slot_depth
    placement = (jnp.arange(slot_count)[:, None] == slot_index[None, :]).astype(jnp.bfloat16)
    normed_assign = jnp.repeat(normed, TOP, axis=0)
    outgoing = jnp.dot(placement, normed_assign, preferred_element_type=jnp.float32).astype(
        jnp.bfloat16
    )
    outgoing = outgoing.reshape(route_count, slot_depth, D)
    incoming = lax.all_to_all(outgoing, ROUTE, split_axis=0, concat_axis=0, tiled=True)
    flat_rows = incoming.reshape(slot_count, D)

    projected = jnp.einsum(
        "qguk,rk->qgur", gate_up_all, flat_rows, preferred_element_type=jnp.float32
    )
    hidden = (jax.nn.silu(projected[:, 0]) * projected[:, 1]).astype(jnp.bfloat16)
    part_out = jnp.einsum("qur,quk->qrk", hidden, down_all, preferred_element_type=jnp.float32)
    part_out = part_out.astype(jnp.bfloat16).astype(jnp.float32)
    summed = part_out[0]
    for quarter in range(1, QUARTERS):
        summed = summed + part_out[quarter]
    summed = summed.astype(jnp.bfloat16).reshape(route_count, slot_depth, D)
    delivered = lax.all_to_all(summed, ROUTE, split_axis=0, concat_axis=0, tiled=True)
    expert_out = lax.dot_general(
        placement,
        delivered.reshape(slot_count, D),
        (((0,), (0,)), ((), ())),
        preferred_element_type=jnp.float32,
    )
    gated = expert_out.reshape(token_rows, TOP, D) * gate_values[0][:, :, None]
    layer_out = (mid_wide + jnp.sum(gated, axis=1)).astype(jnp.bfloat16)
    return layer_out[None]


def solution(mesh):
    ctx_size = mesh.shape["ctx"]
    exp_size = mesh.shape["exp"]
    split_mesh = Mesh(
        mesh.devices.reshape(ctx_size // QUARTERS, QUARTERS // 2, 2, exp_size),
        ("z", "yh", "yl", "e"),
    )
    rows = P("e", CTX, None)
    return jax.shard_map(
        on_device,
        mesh=split_mesh,
        in_specs=(
            rows,
            rows,
            rows,
            rows,
            P(),
            rows,
            rows,
            P(CTX, "e", None, None, None),
            P(CTX, "e", None, None),
        ),
        out_specs=rows,
        check_vma=False,
    )
```

time: 840 us -> 384 us (0.46)
  blocking collectives: 494 us -> 68.7 us
  starting transfers between devices: 227 us -> 21.3 us
  waiting for transfers between devices: 78.1 us -> 236 us
  Pallas kernels: 0 us -> 22.3 us
  local copies, waits for them, and re-layouts: 23.7 us -> 3.06 us
  between operations: 0.24 us -> 13.2 us
    all_to_all x3 -> x1, blocking collectives: 494 us -> 68.7 us  [on_device(): lax.all_to_all(summed, ROUTE, split_axis=0, concat_axis=0, tiled=True)]
    ppermute x31 -> x0, starting transfers between devices: 217 us -> none  [passed_along(): lax.ppermute(value, axis, [(source, source + steps) for source in range(l...]
    all_gather x0 -> x3, waiting for transfers between devices: none -> 183 us  [the longest x1 159 us: on_device(): kv_all = lax.all_gather(own_kv, PROMPT, axis=0, tiled=True)]
    ppermute x31 -> x0, waiting for transfers between devices: 64.2 us -> none  [passed_along(): lax.ppermute(value, axis, [(source, source + steps) for source in range(l...]
    all_to_all x1, waiting for transfers between devices: 14 us -> 51.3 us  [on_device(): lax.all_to_all(outgoing, ROUTE, split_axis=0, concat_axis=0, tiled=True)]
    pallas_call x0 -> x1, Pallas kernels: none -> 22.3 us  [attend(): pl.pallas_call(attend_kernel, out_shape=jax.ShapeDtypeStruct((rows_here,...]
    all_to_all x1, starting transfers between devices: 10.6 us -> 21.2 us  [on_device(): lax.all_to_all(outgoing, ROUTE, split_axis=0, concat_axis=0, tiled=True)]
  transfers between devices with their start and end apart: 32 -> 4, of which waited for: 32 -> 3; matrix products, arithmetic and copies ran while one was open for 0% -> 3% of each run, Pallas kernels for 0% -> 6%
where the time goes in v1:
time: 384 us; the launch traced here: 381 us
  waiting for transfers between devices  236 us (61%)
  blocking collectives  68.7 us (18%)
  Pallas kernels  22.3 us (6%)
  starting transfers between devices  21.3 us (6%)
  between operations  13.2 us (3%)
  matrix products  12.5 us (3%)
  other arithmetic  4.47 us (1%)
    all_gather x1, waiting for transfers between devices, on_device(): kv_all = lax.all_gather(own_kv, PROMPT, axis=0, tiled=True)  159 us
    all_to_all x1, blocking collectives, on_device(): lax.all_to_all(summed, ROUTE, split_axis=0, concat_axis=0, tiled=True)  68.7 us
    all_to_all x1, waiting for transfers between devices, on_device(): lax.all_to_all(outgoing, ROUTE, split_axis=0, concat_axis=0, tiled=True)  51.3 us
    all_gather x1, waiting for transfers between devices, on_device(): down_all = lax.all_gather(w_down[0, 0], QUARTER_AXES, axis=0, tiled=False)  23.6 us
    pallas_call x1, Pallas kernels, attend(): pl.pallas_call(attend_kernel, out_shape=jax.ShapeDtypeStruct((rows_here,...  22.3 us
    all_to_all x1, starting transfers between devices, on_device(): lax.all_to_all(outgoing, ROUTE, split_axis=0, concat_axis=0, tiled=True)  21.2 us
  transfers between devices with their start and end apart: 4, of which 3 were waited for; matrix products, arithmetic and copies ran while one was open for 3% of the time, Pallas kernels for 6%

profile of v1, /device:TPU:1, one launch (start us, length us, event | category | flops | bytes accessed | tf_op | source)
XLA Modules:
  0.0 381.2 jit_solution(4071723408285111727)
XLA Ops:
  6.5 0.0 all-gather.6.cloned.1.call-start
  6.5 1.5 pad_maximum_fusion
  8.1 0.0 all-gather.6.cloned.1.call-update
  8.1 0.0 all-gather.8.cloned.1.call-start
  8.1 0.7 all-gather.8.cloned.1.call-update
  8.9 0.9 fusion.10
  9.8 0.7 convert_add_fusion.1
  10.4 159.4 %all-gather.6.cloned.1.call-done.k_ref.v_ref = bf16[4096,512]{1,0:T(8,128)(2,1)} async-done(((bf16[128,512]{1,0:T(8,128)(2,1)}), bf16[4096,512]{1,0:T(8,128)(2,1)}) %all-gather.6.cloned.1.call-update) | async-done | bytes 4194320 | tf_op jit(solution)/shard_map/all_gather | solution.py:88
  169.8 0.0 copy-start
  169.8 0.0 copy-start.1
  169.8 22.3 %shard_map.91 = f32[128,2048]{1,0:T(8,128)} custom-call(s32[1]{0:T(128)} %bitcast.1.pos_ref, bf16[128,2048]{1,0:T(8,128)(2,1)} %bitcast.44, bf16[4096,512]{1,0:T(8,128)(2,1)} %all-gather.6.cloned.1.call-done.k_ref.v_ref, bf16[4096,512]{1,0:T(8,128)(2,1)} %all-gather.6.cloned.1.call-done.k_ref.v_ref), custom_call_target="tpu_custom_call" | custom-call | flops 4294967296 | bytes 9961472 | tf_op jit(solution)/shard_map/pallas_call | solution.py:56
  192.1 0.0 copy-done
  192.1 1.6 fusion.11
  193.7 0.0 copy-done.1
  193.7 0.5 convolution_convert_fusion
  194.3 1.5 reshape.96
  195.8 21.2 %all-to-all-start = ((bf16[128,2,2048]{2,1,0:T(2,128)(2,1)}), bf16[128,2,2048]{2,1,0:T(2,128)(2,1)S(1)}, u32[]{:S(2)}, u32[]{:S(2)}) async-start(bf16[128,2,2048]{2,1,0:T(2,128)(2,1)} %reshape.96), calls=%async_computation | async-start | bytes 2097152 | tf_op jit(solution)/shard_map/all_to_all | solution.py:119
  217.0 0.0 all-gather.10.cloned.1.call-start
  217.0 0.7 all-gather.10.cloned.1.call-update
  217.7 51.3 %all-to-all-done = bf16[128,2,2048]{2,1,0:T(2,128)(2,1)S(1)} async-done(((bf16[128,2,2048]{2,1,0:T(2,128)(2,1)}), bf16[128,2,2048]{2,1,0:T(2,128)(2,1)S(1)}, u32[]{:S(2)}, u32[]{:S(2)}) %all-to-all-start) | async-done | bytes 1048608 | tf_op jit(solution)/shard_map/all_to_all | solution.py:119
  269.0 0.4 reshape.102
  269.5 0.0 all-gather.8.cloned.1.call-done
  269.5 6.2 %fusion.7 = f32[4,2,192,256]{3,2,1,0:T(8,128)} fusion(bf16[4,1,2,192,2048]{4,3,2,1,0:T(8,128)(2,1)} %all-gather.8.cloned.1.call-done, bf16[256,2048,1,1]{1,0,2,3:T(8,128)(2,1)S(1)} %reshape.102), kind=kOutput, calls=%fused_computation.15 | convolution fusion | flops 1610612736 | bytes 8912896 | tf_op jit(solution)/shard_map/qguk,rk->qgur/dot_general | solution.py:122
  275.7 23.6 %all-gather.10.cloned.1.call-done = bf16[4,1,192,2048]{3,2,1,0:T(8,128)(2,1)} async-done(((bf16[1,1,192,2048]{3,2,1,0:T(8,128)(2,1)}), bf16[4,1,192,2048]{3,2,1,0:T(8,128)(2,1)}) %all-gather.10.cloned.1.call-update) | async-done | bytes 3145744 | tf_op jit(solution)/shard_map/all_gather | solution.py:85
  299.3 3.7 convert_convert_fusion
  303.0 0.7 fusion.6
  303.7 0.0 copy-start.2
  303.7 0.7 convert_element_type.58
  304.4 68.7 %all_to_all.10 = bf16[128,2,2048]{2,1,0:T(2,128)(2,1)S(1)} all-to-all(bf16[128,2,2048]{2,1,0:T(2,128)(2,1)S(1)} %convert_element_type.58), channel_id=1, replica_groups=mesh['z'=16,'yh'=2,'yl'=2,'e'=8] {'z','e'}, dimensions={0} | all-to-all | bytes 2097152 | tf_op jit(solution)/shard_map/all_to_all | solution.py:132
  373.0 0.4 reshape.98
  373.5 0.0 copy-done.2
  373.5 1.2 fusion.5
  (1 shorter events, 0.0 us)
Async XLA Ops:
  6.5 163.3 %all-gather.6.cloned.1.call-start = ((), (), s32[]{:S(2)}) async-start(), calls=%async_computation.2 | async-start | bytes 4325376 | tf_op jit(solution)/shard_map/all_gather | solution.py:88
  8.1 261.4 %all-gather.8.cloned.1.call-start = ((), (), s32[]{:S(2)}) async-start(), calls=%async_computation.3 | async-start | bytes 7864320 | tf_op jit(solution)/shard_map/all_gather | solution.py:84
  169.8 22.3 %copy-start = (bf16[1,128,2048]{2,1,0:T(8,128)(2,1)S(1)}, bf16[1,128,2048]{2,1,0:T(8,128)(2,1)}, u32[]{:S(2)}) copy-start(bf16[1,128,2048]{2,1,0:T(8,128)(2,1)} %param.12) | copy-start | bytes 1572868
  169.8 23.9 %copy-start.1 = (f32[2048]{0:T(1024)S(1)}, f32[2048]{0:T(1024)}, u32[]{:S(2)}) copy-start(f32[2048]{0:T(1024)} %param.13) | copy-start | bytes 24580
  195.8 73.3 %all-to-all-start = ((bf16[128,2,2048]{2,1,0:T(2,128)(2,1)}), bf16[128,2,2048]{2,1,0:T(2,128)(2,1)S(1)}, u32[]{:S(2)}, u32[]{:S(2)}) async-start(bf16[128,2,2048]{2,1,0:T(2,128)(2,1)} %reshape.96), calls=%async_computation | async-start | bytes 2097152 | tf_op jit(solution)/shard_map/all_to_all | solution.py:119
  217.0 82.3 %all-gather.10.cloned.1.call-start = ((), (), s32[]{:S(2)}) async-start(), calls=%async_computation.4 | async-start | bytes 3932160 | tf_op jit(solution)/shard_map/all_gather | solution.py:85
  303.7 69.8 %copy-start.2 = (f32[1,128,1]{1,2,0:T(1,128)S(1)}, f32[1,128,1]{1,2,0:T(1,128)}, u32[]{:S(2)}) copy-start(f32[1,128,1]{1,2,0:T(1,128)} %param.15) | copy-start | bytes 1540
Sparse Core Ops, SparseCore 0:
  10.4 159.3 all-gather.5
  171.9 77.2 all-gather.7
  251.4 47.8 all-gather.9

commit v2 on v1

--- a/solution.py
+++ b/solution.py
@@ -81,11 +81,14 @@
     group_count = lax.axis_size("e")
     per_group = lax.axis_size("z")
 
-    gate_up_all = lax.all_gather(w_gate_up[0, 0], QUARTER_AXES, axis=0, tiled=False)
-    down_all = lax.all_gather(w_down[0, 0], QUARTER_AXES, axis=0, tiled=False)
+    own_kv = jnp.concatenate([rotated_key_rows[0], value_row_array[0]], axis=-1)
+    kv_pair = lax.all_gather(own_kv, "yh", axis=0, tiled=False)
+    kv_all = lax.all_gather(kv_pair, "z", axis=0, tiled=False).reshape(-1, own_kv.shape[-1])
 
-    own_kv = jnp.concatenate([rotated_key_rows[0], value_row_array[0]], axis=-1)
-    kv_all = lax.all_gather(own_kv, PROMPT, axis=0, tiled=True)
+    own_weights = jnp.concatenate([w_gate_up[0, 0], w_down[0, 0][None]], axis=0)
+    weights_all = lax.all_gather(own_weights, QUARTER_AXES, axis=0, tiled=False)
+    gate_up_all = weights_all[:, :2]
+    down_all = weights_all[:, 2]
     pos = (lax.axis_index("z") * lax.axis_size("yh") + lax.axis_index("yh")).astype(jnp.int32)
     attended_rows = attend(pos.reshape(1), queries[0], kv_all)
 

time: 384 us -> 285 us (0.74)
  waiting for transfers between devices: 236 us -> 80 us
  blocking collectives: 68.7 us -> 148 us
  starting transfers between devices: 21.3 us -> 0.04 us
  matrix products: 12.5 us -> 7.97 us
    all_gather x3 -> x2, waiting for transfers between devices: 183 us -> 80 us  [the longest x1 71.2 us: on_device(): lax.all_gather(kv_pair, 'z', axis=0, tiled=False)]
    all_to_all x0 -> x1, blocking collectives: none -> 72.5 us  [on_device(): lax.all_to_all(outgoing, ROUTE, split_axis=0, concat_axis=0, tiled=True)]
    all_to_all x1 -> x0, waiting for transfers between devices: 51.3 us -> none  [on_device(): lax.all_to_all(outgoing, ROUTE, split_axis=0, concat_axis=0, tiled=True)]
    all_to_all x1 -> x0, starting transfers between devices: 21.2 us -> none  [on_device(): lax.all_to_all(outgoing, ROUTE, split_axis=0, concat_axis=0, tiled=True)]
    all_gather x0 -> x1, blocking collectives: none -> 6.85 us  [on_device(): kv_pair = lax.all_gather(own_kv, 'yh', axis=0, tiled=False)]
  transfers between devices with their start and end apart: 4 -> 2, of which waited for: 3 -> 2; matrix products, arithmetic and copies ran while one was open for 3% -> 2% of each run, Pallas kernels for 6% -> 8%
where the time goes in v2:
time: 285 us; the launch traced here: 282 us
  blocking collectives  148 us (52%)
  waiting for transfers between devices  80 us (28%)
  Pallas kernels  22.3 us (8%)
  between operations  13.5 us (5%)
  matrix products  7.97 us (3%)
  other arithmetic  6.29 us (2%)
  local copies, waits for them, and re-layouts  3.62 us (1%)
    all_to_all x1, blocking collectives, on_device(): lax.all_to_all(outgoing, ROUTE, split_axis=0, concat_axis=0, tiled=True)  72.5 us
    all_gather x1, waiting for transfers between devices, on_device(): lax.all_gather(kv_pair, 'z', axis=0, tiled=False)  71.2 us
    all_to_all x1, blocking collectives, on_device(): lax.all_to_all(summed, ROUTE, split_axis=0, concat_axis=0, tiled=True)  68.7 us
    pallas_call x1, Pallas kernels, attend(): pl.pallas_call(attend_kernel, out_shape=jax.ShapeDtypeStruct((rows_here,...  22.3 us
    all_gather x1, waiting for transfers between devices, on_device(): weights_all = lax.all_gather(own_weights, QUARTER_AXES, axis=0, tiled=False)  8.76 us
    all_gather x1, blocking collectives, on_device(): kv_pair = lax.all_gather(own_kv, 'yh', axis=0, tiled=False)  6.85 us
  transfers between devices with their start and end apart: 2, of which 2 were waited for; matrix products, arithmetic and copies ran while one was open for 2% of the time, Pallas kernels for 8%

profile of v2, /device:TPU:1, one launch (start us, length us, event | category | flops | bytes accessed | tf_op | source)
XLA Modules:
  0.0 281.7 jit_solution(5332446804202270970)
XLA Ops:
  6.5 0.0 all-gather.6.cloned.1.call-start
  6.5 0.9 pad_maximum_fusion.1
  7.4 6.8 %all-gather = bf16[256,512]{1,0:T(8,128)(2,1)} all-gather(bf16[128,512]{1,0:T(8,128)(2,1)S(1)} %pad_maximum_fusion.1), channel_id=2, replica_groups=mesh['z'=16,'yh'=2,'yl'=2,'e'=8] {'yh'}, dimensions={0}, use_global_device_ids=true | all-gather | bytes 393216 | tf_op jit(solution)/shard_map/all_gather | solution.py:85
  14.3 0.0 all-gather.6.cloned.1.call-update
  14.3 0.0 all-gather.8.cloned.1.call-start
  14.3 3.2 %pad_maximum_fusion = bf16[3,192,2048]{2,1,0:T(8,128)(2,1)} fusion(bf16[1,192,2048]{2,1,0:T(8,128)(2,1)} %bitcast.44, bf16[2,192,2048]{2,1,0:T(8,128)(2,1)} %bitcast.42), kind=kLoop, calls=%fused_computation.6 | loop fusion | flops 1179648 | bytes 4718592 | tf_op jit(solution)/shard_map/concatenate | solution.py:88
  17.6 0.0 copy-start.4
  17.6 0.0 all-gather.8.cloned.1.call-update
  17.6 0.6 copy-done.4
  18.2 0.2 fusion.4
  18.4 71.2 %all-gather.6.cloned.1.call-done = bf16[32,128,512]{2,1,0:T(8,128)(2,1)} async-done(((bf16[2,128,512]{2,1,0:T(8,128)(2,1)}), bf16[32,128,512]{2,1,0:T(8,128)(2,1)}) %all-gather.6.cloned.1.call-update) | async-done | bytes 4194320 | tf_op jit(solution)/shard_map/all_gather | solution.py:86
  89.6 0.0 copy-start.1
  89.6 0.0 copy-start.2
  89.6 22.3 %shard_map.91 = f32[128,2048]{1,0:T(8,128)} custom-call(s32[1]{0:T(128)} %bitcast.1.pos_ref, bf16[128,2048]{1,0:T(8,128)(2,1)} %bitcast.50, bf16[4096,512]{1,0:T(8,128)(2,1)} %bitcast.48, bf16[4096,512]{1,0:T(8,128)(2,1)} %bitcast.49), custom_call_target="tpu_custom_call" | custom-call | flops 4294967296 | bytes 9961472 | tf_op jit(solution)/shard_map/pallas_call | solution.py:56
  112.0 0.0 copy-done.1
  112.0 1.5 fusion.5
  113.4 0.0 copy-done.2
  113.4 0.5 convolution_convert_fusion
  114.0 0.7 reshape.100
  114.7 72.5 %all_to_all.10 = bf16[128,2,2048]{2,1,0:T(2,128)(2,1)S(1)} all-to-all(bf16[128,2,2048]{2,1,0:T(2,128)(2,1)S(1)} %reshape.100), channel_id=1, replica_groups=mesh['z'=16,'yh'=2,'yl'=2,'e'=8] {'z','e'}, dimensions={0} | all-to-all | bytes 2097152 | tf_op jit(solution)/shard_map/all_to_all | solution.py:122
  187.2 0.4 reshape.108
  187.6 8.8 %all-gather.8.cloned.1.call-done = bf16[12,192,2048]{2,1,0:T(8,128)(2,1)} async-done(((bf16[3,192,2048]{2,1,0:T(8,128)(2,1)}), bf16[12,192,2048]{2,1,0:T(8,128)(2,1)}) %all-gather.8.cloned.1.call-update) | async-done | bytes 9437200 | tf_op jit(solution)/shard_map/all_gather | solution.py:89
  196.4 0.0 copy-start
  196.4 4.8 %fusion.9 = f32[4,2,192,256]{3,2,1,0:T(8,128)S(1)} fusion(bf16[4,3,192,2048]{3,2,1,0:T(8,128)(2,1)} %bitcast.40, bf16[256,2048,1,1]{1,0,2,3:T(8,128)(2,1)S(1)} %reshape.108), kind=kOutput, calls=%fused_computation.21 | convolution fusion | flops 1610612736 | bytes 12058624 | tf_op jit(solution)/shard_map/qguk,rk->qgur/dot_general | solution.py:125
  201.2 0.7 copy-done
  201.9 1.4 convert_convert_fusion
  203.2 0.7 fusion.3
  203.9 0.7 convert_element_type.58
  204.6 0.0 copy-start.3
  204.7 68.7 %all_to_all.11 = bf16[128,2,2048]{2,1,0:T(2,128)(2,1)S(1)} all-to-all(bf16[128,2,2048]{2,1,0:T(2,128)(2,1)S(1)} %convert_element_type.58), channel_id=1, replica_groups=mesh['z'=16,'yh'=2,'yl'=2,'e'=8] {'z','e'}, dimensions={0} | all-to-all | bytes 2097152 | tf_op jit(solution)/shard_map/all_to_all | solution.py:135
  273.3 0.4 reshape.102
  273.7 0.0 copy-done.3
  273.8 1.2 fusion.2
  (2 shorter events, 0.0 us)
Async XLA Ops:
  6.5 83.1 %all-gather.6.cloned.1.call-start = ((), (), s32[]{:S(2)}) async-start(), calls=%async_computation.2 | async-start | bytes 4456448 | tf_op jit(solution)/shard_map/all_gather | solution.py:86
  14.3 182.1 %all-gather.8.cloned.1.call-start = ((), (), s32[]{:S(2)}) async-start(), calls=%async_computation.3 | async-start | bytes 11796480 | tf_op jit(solution)/shard_map/all_gather | solution.py:89
  17.6 0.7 copy-start.4
  89.6 22.3 %copy-start.1 = (bf16[1,128,2048]{2,1,0:T(8,128)(2,1)S(1)}, bf16[1,128,2048]{2,1,0:T(8,128)(2,1)}, u32[]{:S(2)}) copy-start(bf16[1,128,2048]{2,1,0:T(8,128)(2,1)} %param.12) | copy-start | bytes 1572868
  89.6 23.8 %copy-start.2 = (f32[2048]{0:T(1024)S(1)}, f32[2048]{0:T(1024)}, u32[]{:S(2)}) copy-start(f32[2048]{0:T(1024)} %param.13) | copy-start | bytes 24580
  196.4 5.5 %copy-start = (bf16[12,192,2048]{2,1,0:T(8,128)(2,1)S(1)}, bf16[12,192,2048]{2,1,0:T(8,128)(2,1)}, u32[]{:S(2)}) copy-start(bf16[12,192,2048]{2,1,0:T(8,128)(2,1)} %all-gather.8.cloned.1.call-done) | copy-start | bytes 28311556
  204.6 69.1 %copy-start.3 = (f32[1,128,1]{1,2,0:T(1,128)S(1)}, f32[1,128,1]{1,2,0:T(1,128)}, u32[]{:S(2)}) copy-start(f32[1,128,1]{1,2,0:T(1,128)} %param.15) | copy-start | bytes 1540
Sparse Core Ops, SparseCore 0:
  14.4 75.1 all-gather.5
  91.7 104.6 all-gather.7

commit v3 on v2

--- a/solution.py
+++ b/solution.py
@@ -18,21 +18,24 @@
 NEGATIVE_FILL = -1e30
 
 CTX = ("z", "yh", "yl")
-PROMPT = ("z", "yh")
 QUARTER_AXES = ("yh", "yl")
 ROUTE = ("z", "e")
 
 
-def attend_kernel(pos_ref, q_ref, k_ref, v_ref, o_ref):
+def attend_kernel(pos_ref, q_ref, k_ref, v_ref, o_ref, bias_ref):
     rows_here = q_ref.shape[0]
+
+    @pl.when(pl.program_id(0) == 0)
+    def _():
+        query_pos = lax.broadcasted_iota(jnp.int32, bias_ref.shape, 0) + pos_ref[0] * rows_here
+        key_pos = lax.broadcasted_iota(jnp.int32, bias_ref.shape, 1)
+        bias_ref[...] = jnp.where(key_pos <= query_pos, 0.0, NEGATIVE_FILL).astype(jnp.float32)
+
     scores = lax.dot_general(
         q_ref[...], k_ref[...], (((1,), (1,)), ((), ())), preferred_element_type=jnp.float32
-    ) / math.sqrt(HEAD_SIZE)
-    query_pos = lax.broadcasted_iota(jnp.int32, scores.shape, 0) + pos_ref[0] * rows_here
-    key_pos = lax.broadcasted_iota(jnp.int32, scores.shape, 1)
-    scores = jnp.where(key_pos <= query_pos, scores, NEGATIVE_FILL)
+    ) + bias_ref[...]
     row_peak = jnp.max(scores, axis=1, keepdims=True)
-    expo_vals = jnp.exp(scores - row_peak)
+    expo_vals = jnp.exp((scores - row_peak) * (1.0 / math.sqrt(HEAD_SIZE)))
     row_total = jnp.sum(expo_vals, axis=1, keepdims=True)
     summed = jnp.dot(expo_vals.astype(jnp.bfloat16), v_ref[...], preferred_element_type=jnp.float32)
     o_ref[...] = summed / row_total
@@ -52,6 +55,7 @@
             pl.BlockSpec((keys_all, HEAD_SIZE), lambda h, p: (0, KEY_VALUE_HEADS + h // per_kv)),
         ],
         out_specs=pl.BlockSpec((rows_here, HEAD_SIZE), lambda h, p: (0, h)),
+        scratch_shapes=[pltpu.VMEM((rows_here, keys_all), jnp.float32)],
     )
     return pl.pallas_call(
         attend_kernel,
@@ -65,7 +69,7 @@
     )(pos, queries, kv_all, kv_all)
 
 
-def on_device(
+def layer(
     queries,
     rotated_key_rows,
     value_row_array,
@@ -85,10 +89,12 @@
     kv_pair = lax.all_gather(own_kv, "yh", axis=0, tiled=False)
     kv_all = lax.all_gather(kv_pair, "z", axis=0, tiled=False).reshape(-1, own_kv.shape[-1])
 
+    quarter_count = lax.axis_size(QUARTER_AXES)
     own_weights = jnp.concatenate([w_gate_up[0, 0], w_down[0, 0][None]], axis=0)
-    weights_all = lax.all_gather(own_weights, QUARTER_AXES, axis=0, tiled=False)
-    gate_up_all = weights_all[:, :2]
-    down_all = weights_all[:, 2]
+    quarter_weights = [own_weights]
+    for shift in range(1, quarter_count):
+        pairs = [(q, (q + shift) % quarter_count) for q in range(quarter_count)]
+        quarter_weights.append(lax.ppermute(own_weights, QUARTER_AXES, pairs))
     pos = (lax.axis_index("z") * lax.axis_size("yh") + lax.axis_index("yh")).astype(jnp.int32)
     attended_rows = attend(pos.reshape(1), queries[0], kv_all)
 
@@ -122,15 +128,18 @@
     incoming = lax.all_to_all(outgoing, ROUTE, split_axis=0, concat_axis=0, tiled=True)
     flat_rows = incoming.reshape(slot_count, D)
 
-    projected = jnp.einsum(
-        "qguk,rk->qgur", gate_up_all, flat_rows, preferred_element_type=jnp.float32
-    )
-    hidden = (jax.nn.silu(projected[:, 0]) * projected[:, 1]).astype(jnp.bfloat16)
-    part_out = jnp.einsum("qur,quk->qrk", hidden, down_all, preferred_element_type=jnp.float32)
-    part_out = part_out.astype(jnp.bfloat16).astype(jnp.float32)
-    summed = part_out[0]
-    for quarter in range(1, QUARTERS):
-        summed = summed + part_out[quarter]
+    summed = None
+    for weights in quarter_weights:
+        gate_up, down_rows = weights[:2], weights[2]
+        projected = lax.dot_general(
+            gate_up, flat_rows, (((2,), (1,)), ((), ())), preferred_element_type=jnp.float32
+        )
+        hidden = (jax.nn.silu(projected[0]) * projected[1]).astype(jnp.bfloat16)
+        part_out = lax.dot_general(
+            hidden, down_rows, (((0,), (0,)), ((), ())), preferred_element_type=jnp.float32
+        )
+        part_out = part_out.astype(jnp.bfloat16).astype(jnp.float32)
+        summed = part_out if summed is None else summed + part_out
     summed = summed.astype(jnp.bfloat16).reshape(route_count, slot_depth, D)
     delivered = lax.all_to_all(summed, ROUTE, split_axis=0, concat_axis=0, tiled=True)
     expert_out = lax.dot_general(
@@ -153,7 +162,7 @@
     )
     rows = P("e", CTX, None)
     return jax.shard_map(
-        on_device,
+        layer,
         mesh=split_mesh,
         in_specs=(
             rows,

time: 285 us -> 338 us (1.19)
  waiting for transfers between devices: 80 us -> 165 us
  blocking collectives: 148 us -> 76.2 us
  starting transfers between devices: 0.04 us -> 31 us
  matrix products: 7.97 us -> 15.9 us
    all_to_all x2 -> x1, blocking collectives: 141 us -> 69.3 us  [layer(): lax.all_to_all(summed, ROUTE, split_axis=0, concat_axis=0, tiled=True)]
    ppermute x0 -> x3, waiting for transfers between devices: none -> 52.9 us  [layer(): quarter_weights.append(lax.ppermute(own_weights, QUARTER_AXES, pairs))]
    all_to_all x0 -> x1, waiting for transfers between devices: none -> 38.5 us  [layer(): lax.all_to_all(outgoing, ROUTE, split_axis=0, concat_axis=0, tiled=True)]
    all_to_all x0 -> x1, starting transfers between devices: none -> 20.5 us  [layer(): lax.all_to_all(outgoing, ROUTE, split_axis=0, concat_axis=0, tiled=True)]
    ppermute x0 -> x3, starting transfers between devices: none -> 10.5 us  [layer(): quarter_weights.append(lax.ppermute(own_weights, QUARTER_AXES, pairs))]
    dot_general x5 -> x11, matrix products: 7.97 us -> 15.9 us  [the longest x4 8.04 us: layer(): lax.dot_general(gate_up, flat_rows, (((2,), (1,)), ((), ())), preferred_e...]
    all_gather x2 -> x1, waiting for transfers between devices: 80 us -> 73.8 us  [layer(): lax.all_gather(kv_pair, 'z', axis=0, tiled=False)]
  transfers between devices with their start and end apart: 2 -> 5, of which waited for: 2 -> 4; matrix products, arithmetic and copies ran while one was open for 2% -> 3% of each run, Pallas kernels for 8% -> 0%
where the time goes in v3:
time: 338 us; the launch traced here: 334 us
  waiting for transfers between devices  165 us (49%)
  blocking collectives  76.2 us (23%)
  starting transfers between devices  31 us (9%)
  Pallas kernels  23.2 us (7%)
  matrix products  15.9 us (5%)
  between operations  13.6 us (4%)
  other arithmetic  6.04 us (2%)
    all_gather x1, waiting for transfers between devices, layer(): lax.all_gather(kv_pair, 'z', axis=0, tiled=False)  73.8 us
    all_to_all x1, blocking collectives, layer(): lax.all_to_all(summed, ROUTE, split_axis=0, concat_axis=0, tiled=True)  69.3 us
    ppermute x3, waiting for transfers between devices, layer(): quarter_weights.append(lax.ppermute(own_weights, QUARTER_AXES, pairs))  52.9 us
    all_to_all x1, waiting for transfers between devices, layer(): lax.all_to_all(outgoing, ROUTE, split_axis=0, concat_axis=0, tiled=True)  38.5 us
    pallas_call x1, Pallas kernels, attend(): pl.pallas_call(attend_kernel, out_shape=jax.ShapeDtypeStruct((rows_here,...  23.2 us
    all_to_all x1, starting transfers between devices, layer(): lax.all_to_all(outgoing, ROUTE, split_axis=0, concat_axis=0, tiled=True)  20.5 us
    ppermute x3, starting transfers between devices, layer(): quarter_weights.append(lax.ppermute(own_weights, QUARTER_AXES, pairs))  10.5 us
    dot_general x4, matrix products, layer(): lax.dot_general(gate_up, flat_rows, (((2,), (1,)), ((), ())), preferred_e...  8.04 us
  transfers between devices with their start and end apart: 5, of which 4 were waited for; matrix products, arithmetic and copies ran while one was open for 3% of the time, Pallas kernels for 0%

profile of v3, /device:TPU:1, one launch (start us, length us, event | category | flops | bytes accessed | tf_op | source)
XLA Modules:
  0.0 334.2 jit_solution(6551962221241303470)
XLA Ops:
  6.5 0.0 all-gather.4.cloned.1.call-start
  6.5 0.9 pad_maximum_fusion.1
  7.4 6.8 %all-gather = bf16[256,512]{1,0:T(8,128)(2,1)} all-gather(bf16[128,512]{1,0:T(8,128)(2,1)S(1)} %pad_maximum_fusion.1), channel_id=2, replica_groups=mesh['z'=16,'yh'=2,'yl'=2,'e'=8] {'yh'}, dimensions={0}, use_global_device_ids=true | all-gather | bytes 393216 | tf_op jit(solution)/shard_map/all_gather | solution.py:89
  14.3 0.0 all-gather.4.cloned.1.call-update
  14.3 0.9 fusion.11
  15.2 0.7 convert_add_fusion.1
  15.9 73.8 %all-gather.4.cloned.1.call-done = bf16[32,128,512]{2,1,0:T(8,128)(2,1)} async-done(((bf16[2,128,512]{2,1,0:T(8,128)(2,1)}), bf16[32,128,512]{2,1,0:T(8,128)(2,1)}) %all-gather.4.cloned.1.call-update) | async-done | bytes 4194320 | tf_op jit(solution)/shard_map/all_gather | solution.py:90
  89.7 0.0 copy-start.1
  89.7 0.0 copy-start.2
  89.7 23.2 %shard_map.91 = f32[128,2048]{1,0:T(8,128)} custom-call(s32[1]{0:T(128)} %bitcast.1.pos_ref, bf16[128,2048]{1,0:T(8,128)(2,1)} %bitcast.61, bf16[4096,512]{1,0:T(8,128)(2,1)} %bitcast.59, bf16[4096,512]{1,0:T(8,128)(2,1)} %bitcast.60), custom_call_target="tpu_custom_call" | custom-call | flops 4294967296 | bytes 9961472 | tf_op jit(solution)/shard_map/pallas_call | solution.py:60
  112.9 0.0 copy-done.1
  112.9 1.5 fusion.12
  114.4 0.0 copy-done.2
  114.4 0.5 convolution_convert_fusion
  114.9 0.0 copy-start
  114.9 1.5 reshape.98
  116.4 20.5 %all-to-all-start = ((bf16[128,2,2048]{2,1,0:T(2,128)(2,1)}), bf16[128,2,2048]{2,1,0:T(2,128)(2,1)S(1)}, u32[]{:S(2)}, u32[]{:S(2)}) async-start(bf16[128,2,2048]{2,1,0:T(2,128)(2,1)} %reshape.98), calls=%async_computation | async-start | bytes 2097152 | tf_op jit(solution)/shard_map/all_to_all | solution.py:128
  136.9 0.0 copy-done
  136.9 3.0 pad_maximum_fusion
  139.9 3.0 collective-permute-start
  142.9 4.5 %collective-permute-start.1 = (bf16[3,192,2048]{2,1,0:T(8,128)(2,1)}, bf16[3,192,2048]{2,1,0:T(8,128)(2,1)}, u32[]{:S(2)}, u32[]{:S(2)}) collective-permute-start(bf16[3,192,2048]{2,1,0:T(8,128)(2,1)} %pad_maximum_fusion), channel_id=1, source_target_pairs={{0,16},{8,24},{16,0},{24,8},{1,17},{9,25},{17,1},{25,9},{2,18},{10... | collective-permute-start | bytes 7077896 | tf_op jit(solution)/shard_map/ppermute | solution.py:97
  147.3 3.1 collective-permute-start.2
  150.4 38.5 %all-to-all-done = bf16[128,2,2048]{2,1,0:T(2,128)(2,1)S(1)} async-done(((bf16[128,2,2048]{2,1,0:T(2,128)(2,1)}), bf16[128,2,2048]{2,1,0:T(2,128)(2,1)S(1)}, u32[]{:S(2)}, u32[]{:S(2)}) %all-to-all-start) | async-done | bytes 1048608 | tf_op jit(solution)/shard_map/all_to_all | solution.py:128
  188.9 0.4 reshape.106
  189.4 2.0 convolution_bitcast_fusion
  191.4 0.5 fusion.7
  191.9 3.3 collective-permute-done
  195.2 2.0 fusion.43
  197.2 49.5 %collective-permute-done.1 = bf16[3,192,2048]{2,1,0:T(8,128)(2,1)} collective-permute-done((bf16[3,192,2048]{2,1,0:T(8,128)(2,1)}, bf16[3,192,2048]{2,1,0:T(8,128)(2,1)}, u32[]{:S(2)}, u32[]{:S(2)}) %collective-permute-start.1) | collective-permute-done | bytes 2359328 | tf_op jit(solution)/shard_map/ppermute | solution.py:97
  246.7 2.0 fusion.44
  248.8 0.0 collective-permute-done.2
  248.8 2.0 fusion.45
  250.8 1.6 fusion.6
  252.4 1.6 fusion.4
  254.0 1.6 fusion.2
  255.7 0.7 reshape.100
  256.4 0.0 copy-start.3
  256.4 69.3 %all_to_all.10 = bf16[128,2,2048]{2,1,0:T(2,128)(2,1)S(1)} all-to-all(bf16[128,2,2048]{2,1,0:T(2,128)(2,1)S(1)} %reshape.100), channel_id=1, replica_groups=mesh['z'=16,'yh'=2,'yl'=2,'e'=8] {'z','e'}, dimensions={0} | all-to-all | bytes 2097152 | tf_op jit(solution)/shard_map/all_to_all | solution.py:144
  325.7 0.4 reshape.101
  326.2 0.0 copy-done.3
  326.2 1.2 fusion.10
  (1 shorter events, 0.0 us)
Async XLA Ops:
  6.5 83.2 %all-gather.4.cloned.1.call-start = ((), (), s32[]{:S(2)}) async-start(), calls=%async_computation.2 | async-start | bytes 4456448 | tf_op jit(solution)/shard_map/all_gather | solution.py:90
  89.7 23.2 %copy-start.1 = (bf16[1,128,2048]{2,1,0:T(8,128)(2,1)S(1)}, bf16[1,128,2048]{2,1,0:T(8,128)(2,1)}, u32[]{:S(2)}) copy-start(bf16[1,128,2048]{2,1,0:T(8,128)(2,1)} %param.12) | copy-start | bytes 1572868
  89.7 24.7 %copy-start.2 = (f32[2048]{0:T(1024)S(1)}, f32[2048]{0:T(1024)}, u32[]{:S(2)}) copy-start(f32[2048]{0:T(1024)} %param.13) | copy-start | bytes 24580
  114.9 22.0 %copy-start = (bf16[1,1,192,2048]{3,2,1,0:T(8,128)(2,1)S(1)}, bf16[1,1,192,2048]{3,2,1,0:T(8,128)(2,1)}, u32[]{:S(2)}) copy-start(bf16[1,1,192,2048]{3,2,1,0:T(8,128)(2,1)} %param.17) | copy-start | bytes 2359300
  116.4 72.5 %all-to-all-start = ((bf16[128,2,2048]{2,1,0:T(2,128)(2,1)}), bf16[128,2,2048]{2,1,0:T(2,128)(2,1)S(1)}, u32[]{:S(2)}, u32[]{:S(2)}) async-start(bf16[128,2,2048]{2,1,0:T(2,128)(2,1)} %reshape.98), calls=%async_computation | async-start | bytes 2097152 | tf_op jit(solution)/shard_map/all_to_all | solution.py:128
  139.9 55.3 %collective-permute-start = (bf16[3,192,2048]{2,1,0:T(8,128)(2,1)}, bf16[3,192,2048]{2,1,0:T(8,128)(2,1)}, u32[]{:S(2)}, u32[]{:S(2)}) collective-permute-start(bf16[3,192,2048]{2,1,0:T(8,128)(2,1)} %pad_maximum_fusion), channel_id=1, source_target_pairs={{0,8},{8,16},{16,24},{24,0},{1,9},{9,17},{17,25},{25,1},{2,10},{10... | collective-permute-start | bytes 7077896 | tf_op jit(solution)/shard_map/ppermute | solution.py:97
  142.9 103.9 %collective-permute-start.1 = (bf16[3,192,2048]{2,1,0:T(8,128)(2,1)}, bf16[3,192,2048]{2,1,0:T(8,128)(2,1)}, u32[]{:S(2)}, u32[]{:S(2)}) collective-permute-start(bf16[3,192,2048]{2,1,0:T(8,128)(2,1)} %pad_maximum_fusion), channel_id=1, source_target_pairs={{0,16},{8,24},{16,0},{24,8},{1,17},{9,25},{17,1},{25,9},{2,18},{10... | collective-permute-start | bytes 7077896 | tf_op jit(solution)/shard_map/ppermute | solution.py:97
  147.3 101.4 %collective-permute-start.2 = (bf16[3,192,2048]{2,1,0:T(8,128)(2,1)}, bf16[3,192,2048]{2,1,0:T(8,128)(2,1)}, u32[]{:S(2)}, u32[]{:S(2)}) collective-permute-start(bf16[3,192,2048]{2,1,0:T(8,128)(2,1)} %pad_maximum_fusion), channel_id=1, source_target_pairs={{0,24},{8,0},{16,8},{24,16},{1,25},{9,1},{17,9},{25,17},{2,26},{10... | collective-permute-start | bytes 7077896 | tf_op jit(solution)/shard_map/ppermute | solution.py:97
  256.4 69.8 %copy-start.3 = (f32[1,128,1]{1,2,0:T(1,128)S(1)}, f32[1,128,1]{1,2,0:T(1,128)}, u32[]{:S(2)}) copy-start(f32[1,128,1]{1,2,0:T(1,128)} %param.15) | copy-start | bytes 1540
Sparse Core Ops, SparseCore 0:
  14.4 75.2 all-gather.3

commit v4 on v3

--- a/solution.py
+++ b/solution.py
@@ -69,6 +69,54 @@
     )(pos, queries, kv_all, kv_all)
 
 
+def expert_kernel(rows_ref, w0_ref, w1_ref, w2_ref, w3_ref, o_ref, wbuf, sems):
+    hid = w0_ref.shape[1]
+    sources = (w0_ref, w1_ref, w2_ref, w3_ref)
+    copies = [
+        pltpu.make_async_copy(src, wbuf.at[i], sems.at[i]) for i, src in enumerate(sources)
+    ]
+    for copy in copies:
+        copy.start()
+    rows = rows_ref[...]
+    total = None
+    for i, copy in enumerate(copies):
+        copy.wait()
+        gate_up = wbuf[i, 0:2].reshape(2 * hid, rows.shape[1])
+        projected = lax.dot_general(
+            gate_up, rows, (((1,), (1,)), ((), ())), preferred_element_type=jnp.float32
+        )
+        gate, up = projected[:hid], projected[hid:]
+        hidden = (gate / (1.0 + jnp.exp(-gate)) * up).astype(jnp.bfloat16)
+        part_out = lax.dot_general(
+            hidden, wbuf[i, 2], (((0,), (0,)), ((), ())), preferred_element_type=jnp.float32
+        )
+        part_out = part_out.astype(jnp.bfloat16).astype(jnp.float32)
+        total = part_out if total is None else total + part_out
+    o_ref[...] = total.astype(o_ref.dtype)
+
+
+def experts(rows, quarter_weights):
+    count, hid, width = quarter_weights[0].shape
+    slots = rows.shape[0]
+    return pl.pallas_call(
+        expert_kernel,
+        out_shape=jax.ShapeDtypeStruct((slots, width), jnp.bfloat16),
+        in_specs=[pl.BlockSpec(memory_space=pltpu.VMEM)]
+        + [pl.BlockSpec(memory_space=pl.ANY)] * len(quarter_weights),
+        out_specs=pl.BlockSpec(memory_space=pltpu.VMEM),
+        scratch_shapes=[
+            pltpu.VMEM((len(quarter_weights), count, hid, width), jnp.bfloat16),
+            pltpu.SemaphoreType.DMA((len(quarter_weights),)),
+        ],
+        compiler_params=pltpu.CompilerParams(vmem_limit_bytes=48 * 1024 * 1024),
+        cost_estimate=pl.CostEstimate(
+            flops=2 * slots * count * hid * width * len(quarter_weights),
+            transcendentals=slots * hid * len(quarter_weights),
+            bytes_accessed=2 * (count * hid * width * len(quarter_weights) + 2 * slots * width),
+        ),
+    )(rows, *quarter_weights)
+
+
 def layer(
     queries,
     rotated_key_rows,
@@ -128,19 +176,8 @@
     incoming = lax.all_to_all(outgoing, ROUTE, split_axis=0, concat_axis=0, tiled=True)
     flat_rows = incoming.reshape(slot_count, D)
 
-    summed = None
-    for weights in quarter_weights:
-        gate_up, down_rows = weights[:2], weights[2]
-        projected = lax.dot_general(
-            gate_up, flat_rows, (((2,), (1,)), ((), ())), preferred_element_type=jnp.float32
-        )
-        hidden = (jax.nn.silu(projected[0]) * projected[1]).astype(jnp.bfloat16)
-        part_out = lax.dot_general(
-            hidden, down_rows, (((0,), (0,)), ((), ())), preferred_element_type=jnp.float32
-        )
-        part_out = part_out.astype(jnp.bfloat16).astype(jnp.float32)
-        summed = part_out if summed is None else summed + part_out
-    summed = summed.astype(jnp.bfloat16).reshape(route_count, slot_depth, D)
+    summed = experts(flat_rows, quarter_weights)
+    summed = summed.reshape(route_count, slot_depth, D)
     delivered = lax.all_to_all(summed, ROUTE, split_axis=0, concat_axis=0, tiled=True)
     expert_out = lax.dot_general(
         placement,

time: 338 us -> 341 us (level)
  matrix products: 15.9 us -> 2.57 us
  waiting for transfers between devices: 165 us -> 175 us
  Pallas kernels: 23.2 us -> 30.2 us
  local copies, waits for them, and re-layouts: 3.06 us -> 6.96 us
    dot_general x8 -> x0, matrix products: 13.4 us -> none  [the longest x4 8.04 us: layer(): lax.dot_general(gate_up, flat_rows, (((2,), (1,)), ((), ())), preferred_e...]
    ppermute x3, waiting for transfers between devices: 52.9 us -> 60 us  [layer(): quarter_weights.append(lax.ppermute(own_weights, QUARTER_AXES, pairs))]
    pallas_call x0 -> x1, Pallas kernels: none -> 7.03 us  [experts(): pl.pallas_call(expert_kernel, out_shape=jax.ShapeDtypeStruct((slots, widt...]
  transfers between devices with their start and end apart: 5 -> 5, of which waited for: 4 -> 5; matrix products, arithmetic and copies ran while one was open for 3% -> 1% of each run, Pallas kernels for 0% -> 0%
where the time goes in v4:
time: 341 us; the launch traced here: 338 us
  waiting for transfers between devices  175 us (51%)
  blocking collectives  75.1 us (22%)
  starting transfers between devices  30.2 us (9%)
  Pallas kernels  30.2 us (9%)
  between operations  13.5 us (4%)
  local copies, waits for them, and re-layouts  6.96 us (2%)
  other arithmetic  4.64 us (1%)
    all_gather x1, waiting for transfers between devices, layer(): lax.all_gather(kv_pair, 'z', axis=0, tiled=False)  73.8 us
    all_to_all x1, blocking collectives, layer(): lax.all_to_all(summed, ROUTE, split_axis=0, concat_axis=0, tiled=True)  68.2 us
    ppermute x3, waiting for transfers between devices, layer(): quarter_weights.append(lax.ppermute(own_weights, QUARTER_AXES, pairs))  60 us
    all_to_all x1, waiting for transfers between devices, layer(): lax.all_to_all(outgoing, ROUTE, split_axis=0, concat_axis=0, tiled=True)  40.8 us
    pallas_call x1, Pallas kernels, attend(): pl.pallas_call(attend_kernel, out_shape=jax.ShapeDtypeStruct((rows_here,...  23.2 us
    all_to_all x1, starting transfers between devices, layer(): lax.all_to_all(outgoing, ROUTE, split_axis=0, concat_axis=0, tiled=True)  20.9 us
    ppermute x3, starting transfers between devices, layer(): quarter_weights.append(lax.ppermute(own_weights, QUARTER_AXES, pairs))  9.32 us
    pallas_call x1, Pallas kernels, experts(): pl.pallas_call(expert_kernel, out_shape=jax.ShapeDtypeStruct((slots, widt...  7.03 us
  transfers between devices with their start and end apart: 5, of which 5 were waited for; matrix products, arithmetic and copies ran while one was open for 1% of the time, Pallas kernels for 0%

profile of v4, /device:TPU:1, one launch (start us, length us, event | category | flops | bytes accessed | tf_op | source)
XLA Modules:
  0.0 337.8 jit_solution(14479940407793658528)
XLA Ops:
  6.5 0.0 all-gather.4.cloned.1.call-start
  6.5 0.9 pad_maximum_fusion.1
  7.4 6.8 %all-gather = bf16[256,512]{1,0:T(8,128)(2,1)} all-gather(bf16[128,512]{1,0:T(8,128)(2,1)S(1)} %pad_maximum_fusion.1), channel_id=2, replica_groups=mesh['z'=16,'yh'=2,'yl'=2,'e'=8] {'yh'}, dimensions={0}, use_global_device_ids=true | all-gather | bytes 393216 | tf_op jit(solution)/shard_map/all_gather | solution.py:137
  14.3 0.0 all-gather.4.cloned.1.call-update
  14.3 0.9 fusion.3
  15.2 0.7 convert_add_fusion.1
  15.9 73.8 %all-gather.4.cloned.1.call-done = bf16[32,128,512]{2,1,0:T(8,128)(2,1)} async-done(((bf16[2,128,512]{2,1,0:T(8,128)(2,1)}), bf16[32,128,512]{2,1,0:T(8,128)(2,1)}) %all-gather.4.cloned.1.call-update) | async-done | bytes 4194320 | tf_op jit(solution)/shard_map/all_gather | solution.py:138
  89.7 0.0 copy-start.4
  89.7 0.0 copy-start.5
  89.7 23.2 %shard_map.91 = f32[128,2048]{1,0:T(8,128)} custom-call(s32[1]{0:T(128)} %bitcast.1.pos_ref, bf16[128,2048]{1,0:T(8,128)(2,1)} %bitcast.26, bf16[4096,512]{1,0:T(8,128)(2,1)} %bitcast.24, bf16[4096,512]{1,0:T(8,128)(2,1)} %bitcast.25), custom_call_target="tpu_custom_call" | custom-call | flops 4294967296 | bytes 9961472 | tf_op jit(solution)/shard_map/pallas_call | solution.py:60
  112.9 0.0 copy-done.4
  112.9 1.5 fusion.4
  114.3 0.0 copy-start.1
  114.4 0.8 copy-done.1
  115.1 0.0 copy-done.5
  115.1 0.5 convolution_convert_fusion
  115.7 0.0 copy-start.3
  115.7 1.6 reshape.94
  117.2 20.9 %all-to-all-start = ((bf16[128,2,2048]{2,1,0:T(2,128)(2,1)}), bf16[128,2,2048]{2,1,0:T(2,128)(2,1)}, u32[]{:S(2)}, u32[]{:S(2)}) async-start(bf16[128,2,2048]{2,1,0:T(2,128)(2,1)} %reshape.94), calls=%async_computation | async-start | bytes 2097152 | tf_op jit(solution)/shard_map/all_to_all | solution.py:176
  138.2 0.0 copy-done.3
  138.2 1.6 pad_maximum_fusion.w0_ref
  139.8 4.4 %collective-permute-start.2 = (bf16[3,192,2048]{2,1,0:T(8,128)(2,1)S(1)}, bf16[3,192,2048]{2,1,0:T(8,128)(2,1)}, u32[]{:S(2)}, u32[]{:S(2)}) collective-permute-start(bf16[3,192,2048]{2,1,0:T(8,128)(2,1)S(1)} %pad_maximum_fusion.w0_ref), channel_id=1, source_target_pairs={{0,24},{8,0},{16,8},{24,16},{1,25},{9,1},{17,9},{25,17},{2,26},{10... | collective-permute-start | bytes 7077896 | tf_op jit(solution)/shard_map/ppermute | solution.py:145
  144.2 2.3 collective-permute-start.1
  146.5 2.6 collective-permute-start
  149.1 40.8 %all-to-all-done = bf16[128,2,2048]{2,1,0:T(2,128)(2,1)} async-done(((bf16[128,2,2048]{2,1,0:T(2,128)(2,1)}), bf16[128,2,2048]{2,1,0:T(2,128)(2,1)}, u32[]{:S(2)}, u32[]{:S(2)}) %all-to-all-start) | async-done | bytes 1048608 | tf_op jit(solution)/shard_map/all_to_all | solution.py:176
  189.9 1.5 reshape.95.rows_ref
  191.4 3.2 collective-permute-done.2.w3_ref
  194.6 4.7 %collective-permute-done.1.w2_ref = bf16[3,192,2048]{2,1,0:T(8,128)(2,1)} collective-permute-done((bf16[3,192,2048]{2,1,0:T(8,128)(2,1)S(1)}, bf16[3,192,2048]{2,1,0:T(8,128)(2,1)}, u32[]{:S(2)}, u32[]{:S(2)}) %collective-permute-start.1) | collective-permute-done | bytes 2359328 | tf_op jit(solution)/shard_map/ppermute | solution.py:145
  199.3 52.1 %collective-permute-done.w1_ref = bf16[3,192,2048]{2,1,0:T(8,128)(2,1)} collective-permute-done((bf16[3,192,2048]{2,1,0:T(8,128)(2,1)S(1)}, bf16[3,192,2048]{2,1,0:T(8,128)(2,1)}, u32[]{:S(2)}, u32[]{:S(2)}) %collective-permute-start) | collective-permute-done | bytes 2359328 | tf_op jit(solution)/shard_map/ppermute | solution.py:145
  251.4 7.0 %shard_map.92 = bf16[256,2048]{1,0:T(8,128)(2,1)S(1)} custom-call(bf16[256,2048]{1,0:T(8,128)(2,1)S(1)} %reshape.95.rows_ref, bf16[3,192,2048]{2,1,0:T(8,128)(2,1)S(1)} %pad_maximum_fusion.w0_ref, bf16[3,192,2048]{2,1,0:T(8,128)(2,1)} %collective-permute-done.w1_ref, bf16[3,192,2048]{2,1,0:T(8,128)(2,1)} %collective-permute-done.1.w2_ref, ...), custom_call_target="tpu_custom_call" | custom-call | flops 2415919104 | bytes 11534336 | tf_op jit(solution)/shard_map/pallas_call | solution.py:101
  258.4 0.0 copy-start
  258.4 1.0 copy-done
  259.4 1.7 reshape.96
  261.2 0.0 copy-start.2
  261.2 0.0 copy-start.6
  261.2 68.2 %all_to_all.10 = bf16[128,2,2048]{2,1,0:T(2,128)(2,1)S(1)} all-to-all(bf16[128,2,2048]{2,1,0:T(2,128)(2,1)S(1)} %reshape.96), channel_id=1, replica_groups=mesh['z'=16,'yh'=2,'yl'=2,'e'=8] {'z','e'}, dimensions={0} | all-to-all | bytes 2097152 | tf_op jit(solution)/shard_map/all_to_all | solution.py:181
  329.4 0.4 reshape.97
  329.8 0.0 copy-done.2
  329.8 0.0 copy-done.6
  329.8 1.2 fusion.2
  (1 shorter events, 0.0 us)
Async XLA Ops:
  6.5 83.2 %all-gather.4.cloned.1.call-start = ((), (), s32[]{:S(2)}) async-start(), calls=%async_computation.2 | async-start | bytes 4456448 | tf_op jit(solution)/shard_map/all_gather | solution.py:138
  89.7 23.2 %copy-start.4 = (bf16[1,128,2048]{2,1,0:T(8,128)(2,1)S(1)}, bf16[1,128,2048]{2,1,0:T(8,128)(2,1)}, u32[]{:S(2)}) copy-start(bf16[1,128,2048]{2,1,0:T(8,128)(2,1)} %param.12) | copy-start | bytes 1572868
  89.7 25.5 %copy-start.5 = (f32[2048]{0:T(1024)S(1)}, f32[2048]{0:T(1024)}, u32[]{:S(2)}) copy-start(f32[2048]{0:T(1024)} %param.13) | copy-start | bytes 24580
  114.3 0.8 copy-start.1
  115.7 22.5 %copy-start.3 = (bf16[1,1,192,2048]{3,2,1,0:T(8,128)(2,1)S(1)}, bf16[1,1,192,2048]{3,2,1,0:T(8,128)(2,1)}, u32[]{:S(2)}) copy-start(bf16[1,1,192,2048]{3,2,1,0:T(8,128)(2,1)} %param.17) | copy-start | bytes 2359300
  117.2 72.6 %all-to-all-start = ((bf16[128,2,2048]{2,1,0:T(2,128)(2,1)}), bf16[128,2,2048]{2,1,0:T(2,128)(2,1)}, u32[]{:S(2)}, u32[]{:S(2)}) async-start(bf16[128,2,2048]{2,1,0:T(2,128)(2,1)} %reshape.94), calls=%async_computation | async-start | bytes 2097152 | tf_op jit(solution)/shard_map/all_to_all | solution.py:176
  139.8 54.8 %collective-permute-start.2 = (bf16[3,192,2048]{2,1,0:T(8,128)(2,1)S(1)}, bf16[3,192,2048]{2,1,0:T(8,128)(2,1)}, u32[]{:S(2)}, u32[]{:S(2)}) collective-permute-start(bf16[3,192,2048]{2,1,0:T(8,128)(2,1)S(1)} %pad_maximum_fusion.w0_ref), channel_id=1, source_target_pairs={{0,24},{8,0},{16,8},{24,16},{1,25},{9,1},{17,9},{25,17},{2,26},{10... | collective-permute-start | bytes 7077896 | tf_op jit(solution)/shard_map/ppermute | solution.py:145
  144.2 55.1 %collective-permute-start.1 = (bf16[3,192,2048]{2,1,0:T(8,128)(2,1)S(1)}, bf16[3,192,2048]{2,1,0:T(8,128)(2,1)}, u32[]{:S(2)}, u32[]{:S(2)}) collective-permute-start(bf16[3,192,2048]{2,1,0:T(8,128)(2,1)S(1)} %pad_maximum_fusion.w0_ref), channel_id=1, source_target_pairs={{0,16},{8,24},{16,0},{24,8},{1,17},{9,25},{17,1},{25,9},{2,18},{10... | collective-permute-start | bytes 7077896 | tf_op jit(solution)/shard_map/ppermute | solution.py:145
  146.5 104.9 %collective-permute-start = (bf16[3,192,2048]{2,1,0:T(8,128)(2,1)S(1)}, bf16[3,192,2048]{2,1,0:T(8,128)(2,1)}, u32[]{:S(2)}, u32[]{:S(2)}) collective-permute-start(bf16[3,192,2048]{2,1,0:T(8,128)(2,1)S(1)} %pad_maximum_fusion.w0_ref), channel_id=1, source_target_pairs={{0,8},{8,16},{16,24},{24,0},{1,9},{9,17},{17,25},{25,1},{2,10},{10... | collective-permute-start | bytes 7077896 | tf_op jit(solution)/shard_map/ppermute | solution.py:145
  258.4 1.0 copy-start
  261.2 68.7 %copy-start.2 = (bf16[128,2048]{1,0:T(8,128)(2,1)S(1)}, bf16[128,2048]{1,0:T(8,128)(2,1)}, u32[]{:S(2)}) copy-start(bf16[128,2048]{1,0:T(8,128)(2,1)} %copy-done.1) | copy-start | bytes 1572868
  261.2 68.7 %copy-start.6 = (f32[1,128,1]{1,2,0:T(1,128)S(1)}, f32[1,128,1]{1,2,0:T(1,128)}, u32[]{:S(2)}) copy-start(f32[1,128,1]{1,2,0:T(1,128)} %param.15) | copy-start | bytes 1540
Sparse Core Ops, SparseCore 0:
  14.4 75.2 all-gather.3

commit v5 on v4

--- a/solution.py
+++ b/solution.py
@@ -77,30 +77,33 @@
     ]
     for copy in copies:
         copy.start()
-    rows = rows_ref[...]
-    total = None
+    depth = rows_ref.shape[1]
+    planes = [rows_ref[:, s, :] for s in range(depth)]
+    totals = [None] * depth
     for i, copy in enumerate(copies):
         copy.wait()
-        gate_up = wbuf[i, 0:2].reshape(2 * hid, rows.shape[1])
-        projected = lax.dot_general(
-            gate_up, rows, (((1,), (1,)), ((), ())), preferred_element_type=jnp.float32
-        )
-        gate, up = projected[:hid], projected[hid:]
-        hidden = (gate / (1.0 + jnp.exp(-gate)) * up).astype(jnp.bfloat16)
-        part_out = lax.dot_general(
-            hidden, wbuf[i, 2], (((0,), (0,)), ((), ())), preferred_element_type=jnp.float32
-        )
-        part_out = part_out.astype(jnp.bfloat16).astype(jnp.float32)
-        total = part_out if total is None else total + part_out
-    o_ref[...] = total.astype(o_ref.dtype)
+        gate_up = wbuf[i, 0:2].reshape(2 * hid, rows_ref.shape[2])
+        for s, rows in enumerate(planes):
+            projected = lax.dot_general(
+                gate_up, rows, (((1,), (1,)), ((), ())), preferred_element_type=jnp.float32
+            )
+            gate, up = projected[:hid], projected[hid:]
+            hidden = (gate / (1.0 + jnp.exp(-gate)) * up).astype(jnp.bfloat16)
+            part_out = lax.dot_general(
+                hidden, wbuf[i, 2], (((0,), (0,)), ((), ())), preferred_element_type=jnp.float32
+            )
+            part_out = part_out.astype(jnp.bfloat16).astype(jnp.float32)
+            totals[s] = part_out if totals[s] is None else totals[s] + part_out
+    for s in range(depth):
+        o_ref[:, s, :] = totals[s].astype(o_ref.dtype)
 
 
 def experts(rows, quarter_weights):
     count, hid, width = quarter_weights[0].shape
-    slots = rows.shape[0]
+    slots = rows.shape[0] * rows.shape[1]
     return pl.pallas_call(
         expert_kernel,
-        out_shape=jax.ShapeDtypeStruct((slots, width), jnp.bfloat16),
+        out_shape=jax.ShapeDtypeStruct(rows.shape, jnp.bfloat16),
         in_specs=[pl.BlockSpec(memory_space=pltpu.VMEM)]
         + [pl.BlockSpec(memory_space=pl.ANY)] * len(quarter_weights),
         out_specs=pl.BlockSpec(memory_space=pltpu.VMEM),
@@ -169,21 +172,16 @@
     slot_count = route_count * slot_depth
     placement = (jnp.arange(slot_count)[:, None] == slot_index[None, :]).astype(jnp.bfloat16)
     normed_assign = jnp.repeat(normed, TOP, axis=0)
-    outgoing = jnp.dot(placement, normed_assign, preferred_element_type=jnp.float32).astype(
-        jnp.bfloat16
-    )
-    outgoing = outgoing.reshape(route_count, slot_depth, D)
+    placement_3d = placement.reshape(route_count, slot_depth, assign_count)
+    outgoing = jnp.einsum(
+        "dst,tk->dsk", placement_3d, normed_assign, preferred_element_type=jnp.float32
+    ).astype(jnp.bfloat16)
     incoming = lax.all_to_all(outgoing, ROUTE, split_axis=0, concat_axis=0, tiled=True)
-    flat_rows = incoming.reshape(slot_count, D)
-
-    summed = experts(flat_rows, quarter_weights)
-    summed = summed.reshape(route_count, slot_depth, D)
+
+    summed = experts(incoming, quarter_weights)
     delivered = lax.all_to_all(summed, ROUTE, split_axis=0, concat_axis=0, tiled=True)
-    expert_out = lax.dot_general(
-        placement,
-        delivered.reshape(slot_count, D),
-        (((0,), (0,)), ((), ())),
-        preferred_element_type=jnp.float32,
+    expert_out = jnp.einsum(
+        "dst,dsk->tk", placement_3d, delivered, preferred_element_type=jnp.float32
     )
     gated = expert_out.reshape(token_rows, TOP, D) * gate_values[0][:, :, None]
     layer_out = (mid_wide + jnp.sum(gated, axis=1)).astype(jnp.bfloat16)

time: 341 us -> 343 us (level)
  Pallas kernels: 30.2 us -> 35.2 us
    all_to_all x1, waiting for transfers between devices: 40.8 us -> 0.01 us  [layer(): lax.all_to_all(outgoing, ROUTE, split_axis=0, concat_axis=0, tiled=True)]
    ppermute x3, waiting for transfers between devices: 60 us -> 101 us  [layer(): quarter_weights.append(lax.ppermute(own_weights, QUARTER_AXES, pairs))]
    reshape x4 -> x0, local copies, waits for them, and re-layouts: 5.19 us -> none  [the longest x1 1.74 us: layer(): summed = summed.reshape(route_count, slot_depth, D)]
    pallas_call x1, Pallas kernels: 7.03 us -> 12 us  [experts(): pl.pallas_call(expert_kernel, out_shape=jax.ShapeDtypeStruct(rows.shape,...]
  transfers between devices with their start and end apart: 5 -> 5, of which waited for: 5 -> 4; matrix products, arithmetic and copies ran while one was open for 1% -> 1% of each run, Pallas kernels for 0% -> 0%
where the time goes in v5:
time: 343 us; the launch traced here: 340 us
  waiting for transfers between devices  174 us (51%)
  blocking collectives  74.9 us (22%)
  Pallas kernels  35.2 us (10%)
  starting transfers between devices  30 us (9%)
  between operations  13.5 us (4%)
  other arithmetic  4.89 us (1%)
  local copies, waits for them, and re-layouts  4.28 us (1%)
    ppermute x3, waiting for transfers between devices, layer(): quarter_weights.append(lax.ppermute(own_weights, QUARTER_AXES, pairs))  101 us
    all_gather x1, waiting for transfers between devices, layer(): lax.all_gather(kv_pair, 'z', axis=0, tiled=False)  73.8 us
    all_to_all x1, blocking collectives, layer(): lax.all_to_all(summed, ROUTE, split_axis=0, concat_axis=0, tiled=True)  68.1 us
    pallas_call x1, Pallas kernels, attend(): pl.pallas_call(attend_kernel, out_shape=jax.ShapeDtypeStruct((rows_here,...  23.2 us
    all_to_all x1, starting transfers between devices, layer(): lax.all_to_all(outgoing, ROUTE, split_axis=0, concat_axis=0, tiled=True)  20.4 us
    pallas_call x1, Pallas kernels, experts(): pl.pallas_call(expert_kernel, out_shape=jax.ShapeDtypeStruct(rows.shape,...  12 us
    ppermute x3, starting transfers between devices, layer(): quarter_weights.append(lax.ppermute(own_weights, QUARTER_AXES, pairs))  9.51 us
  transfers between devices with their start and end apart: 5, of which 4 were waited for; matrix products, arithmetic and copies ran while one was open for 1% of the time, Pallas kernels for 0%

profile of v5, /device:TPU:1, one launch (start us, length us, event | category | flops | bytes accessed | tf_op | source)
XLA Modules:
  0.0 340.2 jit_solution(17088620218387537242)
XLA Ops:
  6.5 0.0 all-gather.4.cloned.1.call-start
  6.5 0.9 pad_maximum_fusion.1
  7.4 6.8 %all-gather = bf16[256,512]{1,0:T(8,128)(2,1)} all-gather(bf16[128,512]{1,0:T(8,128)(2,1)S(1)} %pad_maximum_fusion.1), channel_id=2, replica_groups=mesh['z'=16,'yh'=2,'yl'=2,'e'=8] {'yh'}, dimensions={0}, use_global_device_ids=true | all-gather | bytes 393216 | tf_op jit(solution)/shard_map/all_gather | solution.py:140
  14.3 0.0 all-gather.4.cloned.1.call-update
  14.3 0.9 fusion.4
  15.2 0.7 convert_add_fusion.1
  15.9 73.8 %all-gather.4.cloned.1.call-done = bf16[32,128,512]{2,1,0:T(8,128)(2,1)} async-done(((bf16[2,128,512]{2,1,0:T(8,128)(2,1)}), bf16[32,128,512]{2,1,0:T(8,128)(2,1)}) %all-gather.4.cloned.1.call-update) | async-done | bytes 4194320 | tf_op jit(solution)/shard_map/all_gather | solution.py:141
  89.7 0.0 copy-start.4
  89.7 0.0 copy-start.5
  89.7 23.2 %shard_map.91 = f32[128,2048]{1,0:T(8,128)} custom-call(s32[1]{0:T(128)} %bitcast.1.pos_ref, bf16[128,2048]{1,0:T(8,128)(2,1)} %bitcast.38, bf16[4096,512]{1,0:T(8,128)(2,1)} %bitcast.36, bf16[4096,512]{1,0:T(8,128)(2,1)} %bitcast.37), custom_call_target="tpu_custom_call" | custom-call | flops 4294967296 | bytes 9961472 | tf_op jit(solution)/shard_map/pallas_call | solution.py:60
  112.9 0.0 copy-done.4
  112.9 1.5 fusion.5
  114.4 0.0 copy-start
  114.4 0.8 copy-done
  115.2 0.0 copy-done.5
  115.2 0.6 fusion.11
  115.7 2.1 copy.16
  117.8 20.4 %all-to-all-start = ((bf16[128,2,2048]{2,1,0:T(2,128)(2,1)}), bf16[128,2,2048]{2,1,0:T(2,128)(2,1)S(1)}, u32[]{:S(2)}, u32[]{:S(2)}) async-start(bf16[128,2,2048]{2,1,0:T(2,128)(2,1)} %copy.16), calls=%async_computation | async-start | bytes 2097152 | tf_op jit(solution)/shard_map/all_to_all | solution.py:179
  138.2 1.9 pad_maximum_fusion.w0_ref
  140.1 0.0 copy-start.6
  140.1 4.4 %collective-permute-start.2 = (bf16[3,192,2048]{2,1,0:T(8,128)(2,1)S(1)}, bf16[3,192,2048]{2,1,0:T(8,128)(2,1)S(1)}, u32[]{:S(2)}, u32[]{:S(2)}) collective-permute-start(bf16[3,192,2048]{2,1,0:T(8,128)(2,1)S(1)} %pad_maximum_fusion.w0_ref), channel_id=1, source_target_pairs={{0,24},{8,0},{16,8},{24,16},{1,25},{9,1},{17,9},{25,17},{2,26},{10... | collective-permute-start | bytes 7077896 | tf_op jit(solution)/shard_map/ppermute | solution.py:148
  144.5 2.3 collective-permute-start.1
  146.8 2.8 collective-permute-start
  149.7 45.3 %collective-permute-done.2.w3_ref = bf16[3,192,2048]{2,1,0:T(8,128)(2,1)S(1)} collective-permute-done((bf16[3,192,2048]{2,1,0:T(8,128)(2,1)S(1)}, bf16[3,192,2048]{2,1,0:T(8,128)(2,1)S(1)}, u32[]{:S(2)}, u32[]{:S(2)}) %collective-permute-start.2) | collective-permute-done | bytes 2359328 | tf_op jit(solution)/shard_map/ppermute | solution.py:148
  195.0 0.0 copy-start.2
  195.0 4.6 %collective-permute-done.1.w2_ref = bf16[3,192,2048]{2,1,0:T(8,128)(2,1)S(1)} collective-permute-done((bf16[3,192,2048]{2,1,0:T(8,128)(2,1)S(1)}, bf16[3,192,2048]{2,1,0:T(8,128)(2,1)S(1)}, u32[]{:S(2)}, u32[]{:S(2)}) %collective-permute-start.1) | collective-permute-done | bytes 2359328 | tf_op jit(solution)/shard_map/ppermute | solution.py:148
  199.6 0.0 copy-done.2
  199.6 0.0 copy-start.3
  199.6 1.4 copy-done.3
  201.0 50.7 %collective-permute-done.w1_ref = bf16[3,192,2048]{2,1,0:T(8,128)(2,1)} collective-permute-done((bf16[3,192,2048]{2,1,0:T(8,128)(2,1)S(1)}, bf16[3,192,2048]{2,1,0:T(8,128)(2,1)}, u32[]{:S(2)}, u32[]{:S(2)}) %collective-permute-start) | collective-permute-done | bytes 2359328 | tf_op jit(solution)/shard_map/ppermute | solution.py:148
  251.7 0.0 all-to-all-done.rows_ref
  251.7 0.0 copy-start.1
  251.7 12.0 %shard_map.92 = bf16[128,2,2048]{2,1,0:T(2,128)(2,1)S(1)} custom-call(bf16[128,2,2048]{2,1,0:T(2,128)(2,1)S(1)} %all-to-all-done.rows_ref, bf16[3,192,2048]{2,1,0:T(8,128)(2,1)S(1)} %pad_maximum_fusion.w0_ref, bf16[3,192,2048]{2,1,0:T(8,128)(2,1)} %collective-permute-done.w1_ref, bf16[3,192,2048]{2,1,0:T(8,128)(2,1)} %copy-done.3, ...), custom_call_target="tpu_custom_call" | custom-call | flops 2415919104 | bytes 11534336 | tf_op jit(solution)/shard_map/pallas_call | solution.py:104
  263.7 68.1 %all_to_all.10 = bf16[128,2,2048]{2,1,0:T(2,128)(2,1)S(1)} all-to-all(bf16[128,2,2048]{2,1,0:T(2,128)(2,1)S(1)} %shard_map.92), channel_id=1, replica_groups=mesh['z'=16,'yh'=2,'yl'=2,'e'=8] {'z','e'}, dimensions={0} | all-to-all | bytes 2097152 | tf_op jit(solution)/shard_map/all_to_all | solution.py:182
  331.8 0.0 copy-done.6
  331.8 0.0 copy-done.1
  331.8 1.6 fusion.3
  (2 shorter events, 0.0 us)
Async XLA Ops:
  6.5 83.2 %all-gather.4.cloned.1.call-start = ((), (), s32[]{:S(2)}) async-start(), calls=%async_computation.2 | async-start | bytes 4456448 | tf_op jit(solution)/shard_map/all_gather | solution.py:141
  89.7 23.2 %copy-start.4 = (bf16[1,128,2048]{2,1,0:T(8,128)(2,1)S(1)}, bf16[1,128,2048]{2,1,0:T(8,128)(2,1)}, u32[]{:S(2)}) copy-start(bf16[1,128,2048]{2,1,0:T(8,128)(2,1)} %param.12) | copy-start | bytes 1572868
  89.7 25.5 %copy-start.5 = (f32[2048]{0:T(1024)S(1)}, f32[2048]{0:T(1024)}, u32[]{:S(2)}) copy-start(f32[2048]{0:T(1024)} %param.13) | copy-start | bytes 24580
  114.4 0.8 copy-start
  117.8 133.9 %all-to-all-start = ((bf16[128,2,2048]{2,1,0:T(2,128)(2,1)}), bf16[128,2,2048]{2,1,0:T(2,128)(2,1)S(1)}, u32[]{:S(2)}, u32[]{:S(2)}) async-start(bf16[128,2,2048]{2,1,0:T(2,128)(2,1)} %copy.16), calls=%async_computation | async-start | bytes 2097152 | tf_op jit(solution)/shard_map/all_to_all | solution.py:179
  140.1 191.7 %copy-start.6 = (f32[1,128,1]{1,2,0:T(1,128)S(1)}, f32[1,128,1]{1,2,0:T(1,128)}, u32[]{:S(2)}) copy-start(f32[1,128,1]{1,2,0:T(1,128)} %param.15) | copy-start | bytes 1540
  140.1 54.9 %collective-permute-start.2 = (bf16[3,192,2048]{2,1,0:T(8,128)(2,1)S(1)}, bf16[3,192,2048]{2,1,0:T(8,128)(2,1)S(1)}, u32[]{:S(2)}, u32[]{:S(2)}) collective-permute-start(bf16[3,192,2048]{2,1,0:T(8,128)(2,1)S(1)} %pad_maximum_fusion.w0_ref), channel_id=1, source_target_pairs={{0,24},{8,0},{16,8},{24,16},{1,25},{9,1},{17,9},{25,17},{2,26},{10... | collective-permute-start | bytes 7077896 | tf_op jit(solution)/shard_map/ppermute | solution.py:148
  144.5 55.1 %collective-permute-start.1 = (bf16[3,192,2048]{2,1,0:T(8,128)(2,1)S(1)}, bf16[3,192,2048]{2,1,0:T(8,128)(2,1)S(1)}, u32[]{:S(2)}, u32[]{:S(2)}) collective-permute-start(bf16[3,192,2048]{2,1,0:T(8,128)(2,1)S(1)} %pad_maximum_fusion.w0_ref), channel_id=1, source_target_pairs={{0,16},{8,24},{16,0},{24,8},{1,17},{9,25},{17,1},{25,9},{2,18},{10... | collective-permute-start | bytes 7077896 | tf_op jit(solution)/shard_map/ppermute | solution.py:148
  146.8 104.9 %collective-permute-start = (bf16[3,192,2048]{2,1,0:T(8,128)(2,1)S(1)}, bf16[3,192,2048]{2,1,0:T(8,128)(2,1)}, u32[]{:S(2)}, u32[]{:S(2)}) collective-permute-start(bf16[3,192,2048]{2,1,0:T(8,128)(2,1)S(1)} %pad_maximum_fusion.w0_ref), channel_id=1, source_target_pairs={{0,8},{8,16},{16,24},{24,0},{1,9},{9,17},{17,25},{25,1},{2,10},{10... | collective-permute-start | bytes 7077896 | tf_op jit(solution)/shard_map/ppermute | solution.py:148
  195.0 4.6 %copy-start.2 = (bf16[3,192,2048]{2,1,0:T(8,128)(2,1)}, bf16[3,192,2048]{2,1,0:T(8,128)(2,1)S(1)}, u32[]{:S(2)}) copy-start(bf16[3,192,2048]{2,1,0:T(8,128)(2,1)S(1)} %collective-permute-done.2.w3_ref) | copy-start | bytes 7077892
  199.6 1.4 copy-start.3
  251.7 80.1 %copy-start.1 = (bf16[128,2048]{1,0:T(8,128)(2,1)S(1)}, bf16[128,2048]{1,0:T(8,128)(2,1)}, u32[]{:S(2)}) copy-start(bf16[128,2048]{1,0:T(8,128)(2,1)} %copy-done) | copy-start | bytes 1572868
Sparse Core Ops, SparseCore 0:
  14.4 75.2 all-gather.3

commit v6 on v4

--- a/solution.py
+++ b/solution.py
@@ -22,20 +22,16 @@
 ROUTE = ("z", "e")
 
 
-def attend_kernel(pos_ref, q_ref, k_ref, v_ref, o_ref, bias_ref):
+def attend_kernel(pos_ref, q_ref, k_ref, v_ref, o_ref):
     rows_here = q_ref.shape[0]
-
-    @pl.when(pl.program_id(0) == 0)
-    def _():
-        query_pos = lax.broadcasted_iota(jnp.int32, bias_ref.shape, 0) + pos_ref[0] * rows_here
-        key_pos = lax.broadcasted_iota(jnp.int32, bias_ref.shape, 1)
-        bias_ref[...] = jnp.where(key_pos <= query_pos, 0.0, NEGATIVE_FILL).astype(jnp.float32)
-
     scores = lax.dot_general(
         q_ref[...], k_ref[...], (((1,), (1,)), ((), ())), preferred_element_type=jnp.float32
-    ) + bias_ref[...]
+    ) / math.sqrt(HEAD_SIZE)
+    query_pos = lax.broadcasted_iota(jnp.int32, scores.shape, 0) + pos_ref[0] * rows_here
+    key_pos = lax.broadcasted_iota(jnp.int32, scores.shape, 1)
+    scores = jnp.where(key_pos <= query_pos, scores, NEGATIVE_FILL)
     row_peak = jnp.max(scores, axis=1, keepdims=True)
-    expo_vals = jnp.exp((scores - row_peak) * (1.0 / math.sqrt(HEAD_SIZE)))
+    expo_vals = jnp.exp(scores - row_peak)
     row_total = jnp.sum(expo_vals, axis=1, keepdims=True)
     summed = jnp.dot(expo_vals.astype(jnp.bfloat16), v_ref[...], preferred_element_type=jnp.float32)
     o_ref[...] = summed / row_total
@@ -55,7 +51,6 @@
             pl.BlockSpec((keys_all, HEAD_SIZE), lambda h, p: (0, KEY_VALUE_HEADS + h // per_kv)),
         ],
         out_specs=pl.BlockSpec((rows_here, HEAD_SIZE), lambda h, p: (0, h)),
-        scratch_shapes=[pltpu.VMEM((rows_here, keys_all), jnp.float32)],
     )
     return pl.pallas_call(
         attend_kernel,

time: 341 us -> 340 us (level)
  no operation moved by 1% of the time
where the time goes in v6:
time: 340 us; the launch traced here: 337 us
  waiting for transfers between devices  175 us (51%)
  blocking collectives  75.1 us (22%)
  starting transfers between devices  30.2 us (9%)
  Pallas kernels  29.3 us (9%)
  between operations  13.5 us (4%)
  local copies, waits for them, and re-layouts  6.96 us (2%)
  other arithmetic  4.64 us (1%)
    all_gather x1, waiting for transfers between devices, layer(): lax.all_gather(kv_pair, 'z', axis=0, tiled=False)  73.8 us
    all_to_all x1, blocking collectives, layer(): lax.all_to_all(summed, ROUTE, split_axis=0, concat_axis=0, tiled=True)  68.2 us
    ppermute x3, waiting for transfers between devices, layer(): quarter_weights.append(lax.ppermute(own_weights, QUARTER_AXES, pairs))  60 us
    all_to_all x1, waiting for transfers between devices, layer(): lax.all_to_all(outgoing, ROUTE, split_axis=0, concat_axis=0, tiled=True)  40.8 us
    pallas_call x1, Pallas kernels, attend(): pl.pallas_call(attend_kernel, out_shape=jax.ShapeDtypeStruct((rows_here,...  22.3 us
    all_to_all x1, starting transfers between devices, layer(): lax.all_to_all(outgoing, ROUTE, split_axis=0, concat_axis=0, tiled=True)  20.9 us
    ppermute x3, starting transfers between devices, layer(): quarter_weights.append(lax.ppermute(own_weights, QUARTER_AXES, pairs))  9.32 us
    pallas_call x1, Pallas kernels, experts(): pl.pallas_call(expert_kernel, out_shape=jax.ShapeDtypeStruct((slots, widt...  7.03 us
  transfers between devices with their start and end apart: 5, of which 5 were waited for; matrix products, arithmetic and copies ran while one was open for 1% of the time, Pallas kernels for 0%

profile of v6, /device:TPU:1, one launch (start us, length us, event | category | flops | bytes accessed | tf_op | source)
XLA Modules:
  0.0 336.9 jit_solution(9093409381017529065)
XLA Ops:
  6.5 0.0 all-gather.4.cloned.1.call-start
  6.5 0.9 pad_maximum_fusion.1
  7.4 6.8 %all-gather = bf16[256,512]{1,0:T(8,128)(2,1)} all-gather(bf16[128,512]{1,0:T(8,128)(2,1)S(1)} %pad_maximum_fusion.1), channel_id=2, replica_groups=mesh['z'=16,'yh'=2,'yl'=2,'e'=8] {'yh'}, dimensions={0}, use_global_device_ids=true | all-gather | bytes 393216 | tf_op jit(solution)/shard_map/all_gather | solution.py:132
  14.3 0.0 all-gather.4.cloned.1.call-update
  14.3 0.9 fusion.3
  15.2 0.7 convert_add_fusion.1
  15.9 73.8 %all-gather.4.cloned.1.call-done = bf16[32,128,512]{2,1,0:T(8,128)(2,1)} async-done(((bf16[2,128,512]{2,1,0:T(8,128)(2,1)}), bf16[32,128,512]{2,1,0:T(8,128)(2,1)}) %all-gather.4.cloned.1.call-update) | async-done | bytes 4194320 | tf_op jit(solution)/shard_map/all_gather | solution.py:133
  89.7 0.0 copy-start.4
  89.7 0.0 copy-start.5
  89.7 22.3 %shard_map.91 = f32[128,2048]{1,0:T(8,128)} custom-call(s32[1]{0:T(128)} %bitcast.1.pos_ref, bf16[128,2048]{1,0:T(8,128)(2,1)} %bitcast.26, bf16[4096,512]{1,0:T(8,128)(2,1)} %bitcast.24, bf16[4096,512]{1,0:T(8,128)(2,1)} %bitcast.25), custom_call_target="tpu_custom_call" | custom-call | flops 4294967296 | bytes 9961472 | tf_op jit(solution)/shard_map/pallas_call | solution.py:55
  112.0 0.0 copy-done.4
  112.0 1.5 fusion.4
  113.4 0.0 copy-start.1
  113.5 0.8 copy-done.1
  114.2 0.0 copy-done.5
  114.2 0.5 convolution_convert_fusion
  114.8 0.0 copy-start.3
  114.8 1.6 reshape.94
  116.3 20.9 %all-to-all-start = ((bf16[128,2,2048]{2,1,0:T(2,128)(2,1)}), bf16[128,2,2048]{2,1,0:T(2,128)(2,1)}, u32[]{:S(2)}, u32[]{:S(2)}) async-start(bf16[128,2,2048]{2,1,0:T(2,128)(2,1)} %reshape.94), calls=%async_computation | async-start | bytes 2097152 | tf_op jit(solution)/shard_map/all_to_all | solution.py:171
  137.2 0.0 copy-done.3
  137.2 1.6 pad_maximum_fusion.w0_ref
  138.9 4.4 %collective-permute-start.2 = (bf16[3,192,2048]{2,1,0:T(8,128)(2,1)S(1)}, bf16[3,192,2048]{2,1,0:T(8,128)(2,1)}, u32[]{:S(2)}, u32[]{:S(2)}) collective-permute-start(bf16[3,192,2048]{2,1,0:T(8,128)(2,1)S(1)} %pad_maximum_fusion.w0_ref), channel_id=1, source_target_pairs={{0,24},{8,0},{16,8},{24,16},{1,25},{9,1},{17,9},{25,17},{2,26},{10... | collective-permute-start | bytes 7077896 | tf_op jit(solution)/shard_map/ppermute | solution.py:140
  143.2 2.3 collective-permute-start.1
  145.6 2.6 collective-permute-start
  148.2 40.8 %all-to-all-done = bf16[128,2,2048]{2,1,0:T(2,128)(2,1)} async-done(((bf16[128,2,2048]{2,1,0:T(2,128)(2,1)}), bf16[128,2,2048]{2,1,0:T(2,128)(2,1)}, u32[]{:S(2)}, u32[]{:S(2)}) %all-to-all-start) | async-done | bytes 1048608 | tf_op jit(solution)/shard_map/all_to_all | solution.py:171
  189.0 1.5 reshape.95.rows_ref
  190.4 3.2 collective-permute-done.2.w3_ref
  193.6 4.7 %collective-permute-done.1.w2_ref = bf16[3,192,2048]{2,1,0:T(8,128)(2,1)} collective-permute-done((bf16[3,192,2048]{2,1,0:T(8,128)(2,1)S(1)}, bf16[3,192,2048]{2,1,0:T(8,128)(2,1)}, u32[]{:S(2)}, u32[]{:S(2)}) %collective-permute-start.1) | collective-permute-done | bytes 2359328 | tf_op jit(solution)/shard_map/ppermute | solution.py:140
  198.3 52.1 %collective-permute-done.w1_ref = bf16[3,192,2048]{2,1,0:T(8,128)(2,1)} collective-permute-done((bf16[3,192,2048]{2,1,0:T(8,128)(2,1)S(1)}, bf16[3,192,2048]{2,1,0:T(8,128)(2,1)}, u32[]{:S(2)}, u32[]{:S(2)}) %collective-permute-start) | collective-permute-done | bytes 2359328 | tf_op jit(solution)/shard_map/ppermute | solution.py:140
  250.5 7.0 %shard_map.92 = bf16[256,2048]{1,0:T(8,128)(2,1)S(1)} custom-call(bf16[256,2048]{1,0:T(8,128)(2,1)S(1)} %reshape.95.rows_ref, bf16[3,192,2048]{2,1,0:T(8,128)(2,1)S(1)} %pad_maximum_fusion.w0_ref, bf16[3,192,2048]{2,1,0:T(8,128)(2,1)} %collective-permute-done.w1_ref, bf16[3,192,2048]{2,1,0:T(8,128)(2,1)} %collective-permute-done.1.w2_ref, ...), custom_call_target="tpu_custom_call" | custom-call | flops 2415919104 | bytes 11534336 | tf_op jit(solution)/shard_map/pallas_call | solution.py:96
  257.5 0.0 copy-start
  257.5 1.0 copy-done
  258.5 1.7 reshape.96
  260.2 0.0 copy-start.2
  260.3 0.0 copy-start.6
  260.3 68.2 %all_to_all.10 = bf16[128,2,2048]{2,1,0:T(2,128)(2,1)S(1)} all-to-all(bf16[128,2,2048]{2,1,0:T(2,128)(2,1)S(1)} %reshape.96), channel_id=1, replica_groups=mesh['z'=16,'yh'=2,'yl'=2,'e'=8] {'z','e'}, dimensions={0} | all-to-all | bytes 2097152 | tf_op jit(solution)/shard_map/all_to_all | solution.py:176
  328.5 0.4 reshape.97
  328.9 0.0 copy-done.2
  328.9 0.0 copy-done.6
  328.9 1.2 fusion.2
  (1 shorter events, 0.0 us)
Async XLA Ops:
  6.5 83.2 %all-gather.4.cloned.1.call-start = ((), (), s32[]{:S(2)}) async-start(), calls=%async_computation.2 | async-start | bytes 4456448 | tf_op jit(solution)/shard_map/all_gather | solution.py:133
  89.7 22.3 %copy-start.4 = (bf16[1,128,2048]{2,1,0:T(8,128)(2,1)S(1)}, bf16[1,128,2048]{2,1,0:T(8,128)(2,1)}, u32[]{:S(2)}) copy-start(bf16[1,128,2048]{2,1,0:T(8,128)(2,1)} %param.12) | copy-start | bytes 1572868
  89.7 24.5 %copy-start.5 = (f32[2048]{0:T(1024)S(1)}, f32[2048]{0:T(1024)}, u32[]{:S(2)}) copy-start(f32[2048]{0:T(1024)} %param.13) | copy-start | bytes 24580
  113.4 0.8 copy-start.1
  114.8 22.5 %copy-start.3 = (bf16[1,1,192,2048]{3,2,1,0:T(8,128)(2,1)S(1)}, bf16[1,1,192,2048]{3,2,1,0:T(8,128)(2,1)}, u32[]{:S(2)}) copy-start(bf16[1,1,192,2048]{3,2,1,0:T(8,128)(2,1)} %param.17) | copy-start | bytes 2359300
  116.3 72.6 %all-to-all-start = ((bf16[128,2,2048]{2,1,0:T(2,128)(2,1)}), bf16[128,2,2048]{2,1,0:T(2,128)(2,1)}, u32[]{:S(2)}, u32[]{:S(2)}) async-start(bf16[128,2,2048]{2,1,0:T(2,128)(2,1)} %reshape.94), calls=%async_computation | async-start | bytes 2097152 | tf_op jit(solution)/shard_map/all_to_all | solution.py:171
  138.9 54.8 %collective-permute-start.2 = (bf16[3,192,2048]{2,1,0:T(8,128)(2,1)S(1)}, bf16[3,192,2048]{2,1,0:T(8,128)(2,1)}, u32[]{:S(2)}, u32[]{:S(2)}) collective-permute-start(bf16[3,192,2048]{2,1,0:T(8,128)(2,1)S(1)} %pad_maximum_fusion.w0_ref), channel_id=1, source_target_pairs={{0,24},{8,0},{16,8},{24,16},{1,25},{9,1},{17,9},{25,17},{2,26},{10... | collective-permute-start | bytes 7077896 | tf_op jit(solution)/shard_map/ppermute | solution.py:140
  143.2 55.1 %collective-permute-start.1 = (bf16[3,192,2048]{2,1,0:T(8,128)(2,1)S(1)}, bf16[3,192,2048]{2,1,0:T(8,128)(2,1)}, u32[]{:S(2)}, u32[]{:S(2)}) collective-permute-start(bf16[3,192,2048]{2,1,0:T(8,128)(2,1)S(1)} %pad_maximum_fusion.w0_ref), channel_id=1, source_target_pairs={{0,16},{8,24},{16,0},{24,8},{1,17},{9,25},{17,1},{25,9},{2,18},{10... | collective-permute-start | bytes 7077896 | tf_op jit(solution)/shard_map/ppermute | solution.py:140
  145.6 104.9 %collective-permute-start = (bf16[3,192,2048]{2,1,0:T(8,128)(2,1)S(1)}, bf16[3,192,2048]{2,1,0:T(8,128)(2,1)}, u32[]{:S(2)}, u32[]{:S(2)}) collective-permute-start(bf16[3,192,2048]{2,1,0:T(8,128)(2,1)S(1)} %pad_maximum_fusion.w0_ref), channel_id=1, source_target_pairs={{0,8},{8,16},{16,24},{24,0},{1,9},{9,17},{17,25},{25,1},{2,10},{10... | collective-permute-start | bytes 7077896 | tf_op jit(solution)/shard_map/ppermute | solution.py:140
  257.5 1.0 copy-start
  260.2 68.7 %copy-start.2 = (bf16[128,2048]{1,0:T(8,128)(2,1)S(1)}, bf16[128,2048]{1,0:T(8,128)(2,1)}, u32[]{:S(2)}) copy-start(bf16[128,2048]{1,0:T(8,128)(2,1)} %copy-done.1) | copy-start | bytes 1572868
  260.3 68.7 %copy-start.6 = (f32[1,128,1]{1,2,0:T(1,128)S(1)}, f32[1,128,1]{1,2,0:T(1,128)}, u32[]{:S(2)}) copy-start(f32[1,128,1]{1,2,0:T(1,128)} %param.15) | copy-start | bytes 1540
Sparse Core Ops, SparseCore 0:
  14.4 75.2 all-gather.3

commit v7 on v6

--- a/solution.py
+++ b/solution.py
@@ -22,7 +22,7 @@
 ROUTE = ("z", "e")
 
 
-def attend_kernel(pos_ref, q_ref, k_ref, v_ref, o_ref):
+def attend_kernel(pos_ref, q_ref, k_ref, v_ref, res_ref, o_ref):
     rows_here = q_ref.shape[0]
     scores = lax.dot_general(
         q_ref[...], k_ref[...], (((1,), (1,)), ((), ())), preferred_element_type=jnp.float32
@@ -34,10 +34,10 @@
     expo_vals = jnp.exp(scores - row_peak)
     row_total = jnp.sum(expo_vals, axis=1, keepdims=True)
     summed = jnp.dot(expo_vals.astype(jnp.bfloat16), v_ref[...], preferred_element_type=jnp.float32)
-    o_ref[...] = summed / row_total
-
-
-def attend(pos, queries, kv_all):
+    o_ref[...] = (res_ref[...].astype(jnp.float32) + summed / row_total).astype(o_ref.dtype)
+
+
+def attend(pos, queries, kv_all, residual_rows):
     rows_here = queries.shape[0]
     keys_all = kv_all.shape[0]
     per_kv = QUERY_HEADS // KEY_VALUE_HEADS
@@ -49,19 +49,20 @@
             pl.BlockSpec((rows_here, HEAD_SIZE), lambda h, p: (0, h)),
             pl.BlockSpec((keys_all, HEAD_SIZE), lambda h, p: (0, h // per_kv)),
             pl.BlockSpec((keys_all, HEAD_SIZE), lambda h, p: (0, KEY_VALUE_HEADS + h // per_kv)),
+            pl.BlockSpec((rows_here, HEAD_SIZE), lambda h, p: (0, h)),
         ],
         out_specs=pl.BlockSpec((rows_here, HEAD_SIZE), lambda h, p: (0, h)),
     )
     return pl.pallas_call(
         attend_kernel,
-        out_shape=jax.ShapeDtypeStruct((rows_here, QUERY_HEADS * HEAD_SIZE), jnp.float32),
+        out_shape=jax.ShapeDtypeStruct((rows_here, QUERY_HEADS * HEAD_SIZE), jnp.bfloat16),
         grid_spec=grid_spec,
         cost_estimate=pl.CostEstimate(
             flops=flops,
             transcendentals=QUERY_HEADS * rows_here * keys_all,
             bytes_accessed=2 * kv_all.size * 2 + queries.size * 2 + rows_here * D * 4,
         ),
-    )(pos, queries, kv_all, kv_all)
+    )(pos, queries, kv_all, kv_all, residual_rows)
 
 
 def expert_kernel(rows_ref, w0_ref, w1_ref, w2_ref, w3_ref, o_ref, wbuf, sems):
@@ -139,9 +140,8 @@
         pairs = [(q, (q + shift) % quarter_count) for q in range(quarter_count)]
         quarter_weights.append(lax.ppermute(own_weights, QUARTER_AXES, pairs))
     pos = (lax.axis_index("z") * lax.axis_size("yh") + lax.axis_index("yh")).astype(jnp.int32)
-    attended_rows = attend(pos.reshape(1), queries[0], kv_all)
-
-    mid_rows = (residual[0].astype(jnp.float32) + attended_rows).astype(jnp.bfloat16)
+    mid_rows = attend(pos.reshape(1), queries[0], kv_all, residual[0])
+
     mid_wide = mid_rows.astype(jnp.float32)
     inverse = lax.rsqrt(jnp.mean(mid_wide * mid_wide, axis=-1, keepdims=True) + 1e-06)
     normed = (mid_wide * inverse * norm_gain).astype(jnp.bfloat16)

time: 340 us -> 340 us (level)
  no operation moved by 1% of the time
where the time goes in v7:
time: 340 us; the launch traced here: 337 us
  waiting for transfers between devices  175 us (51%)
  blocking collectives  75.1 us (22%)
  starting transfers between devices  30.2 us (9%)
  Pallas kernels  29.4 us (9%)
  between operations  13.5 us (4%)
  local copies, waits for them, and re-layouts  6.17 us (2%)
  other arithmetic  4.41 us (1%)
  matrix products  3.61 us (1%)
    all_gather x1, waiting for transfers between devices, layer(): lax.all_gather(kv_pair, 'z', axis=0, tiled=False)  73.8 us
    all_to_all x1, blocking collectives, layer(): lax.all_to_all(summed, ROUTE, split_axis=0, concat_axis=0, tiled=True)  68.2 us
    ppermute x3, waiting for transfers between devices, layer(): quarter_weights.append(lax.ppermute(own_weights, QUARTER_AXES, pairs))  60 us
    all_to_all x1, waiting for transfers between devices, layer(): lax.all_to_all(outgoing, ROUTE, split_axis=0, concat_axis=0, tiled=True)  40.7 us
    pallas_call x1, Pallas kernels, attend(): pl.pallas_call(attend_kernel, out_shape=jax.ShapeDtypeStruct((rows_here,...  22.4 us
    all_to_all x1, starting transfers between devices, layer(): lax.all_to_all(outgoing, ROUTE, split_axis=0, concat_axis=0, tiled=True)  20.9 us
    ppermute x3, starting transfers between devices, layer(): quarter_weights.append(lax.ppermute(own_weights, QUARTER_AXES, pairs))  9.32 us
    pallas_call x1, Pallas kernels, experts(): pl.pallas_call(expert_kernel, out_shape=jax.ShapeDtypeStruct((slots, widt...  7.03 us
  transfers between devices with their start and end apart: 5, of which 5 were waited for; matrix products, arithmetic and copies ran while one was open for 1% of the time, Pallas kernels for 0%

profile of v7, /device:TPU:1, one launch (start us, length us, event | category | flops | bytes accessed | tf_op | source)
XLA Modules:
  0.0 337.0 jit_solution(12024970896370267337)
XLA Ops:
  6.5 0.0 all-gather.4.cloned.1.call-start
  6.5 0.9 pad_maximum_fusion.1
  7.4 6.8 %all-gather = bf16[256,512]{1,0:T(8,128)(2,1)} all-gather(bf16[128,512]{1,0:T(8,128)(2,1)S(1)} %pad_maximum_fusion.1), channel_id=2, replica_groups=mesh['z'=16,'yh'=2,'yl'=2,'e'=8] {'yh'}, dimensions={0}, use_global_device_ids=true | all-gather | bytes 393216 | tf_op jit(solution)/shard_map/all_gather | solution.py:133
  14.3 0.0 all-gather.4.cloned.1.call-update
  14.3 0.9 fusion.3
  15.2 0.7 convert_add_fusion
  15.9 73.8 %all-gather.4.cloned.1.call-done = bf16[32,128,512]{2,1,0:T(8,128)(2,1)} async-done(((bf16[2,128,512]{2,1,0:T(8,128)(2,1)}), bf16[32,128,512]{2,1,0:T(8,128)(2,1)}) %all-gather.4.cloned.1.call-update) | async-done | bytes 4194320 | tf_op jit(solution)/shard_map/all_gather | solution.py:134
  89.7 0.0 copy-start.3
  89.7 22.4 %shard_map.91 = bf16[128,2048]{1,0:T(8,128)(2,1)} custom-call(s32[1]{0:T(128)} %bitcast.pos_ref, bf16[128,2048]{1,0:T(8,128)(2,1)} %bitcast.23, bf16[4096,512]{1,0:T(8,128)(2,1)} %bitcast.21, bf16[4096,512]{1,0:T(8,128)(2,1)} %bitcast.22, bf16[128,2048]{1,0:T(8,128)(2,1)} %bitcast.24), custom_call_target="tpu_custom_call" | custom-call | flops 4294967296 | bytes 9961472 | tf_op jit(solution)/shard_map/pallas_call | solution.py:56
  112.1 1.2 fusion.4
  113.3 0.0 copy-done.3
  113.3 1.5 convolution_convert_fusion
  114.9 0.0 copy-start.2
  114.9 1.6 reshape.92
  116.4 20.9 %all-to-all-start = ((bf16[128,2,2048]{2,1,0:T(2,128)(2,1)}), bf16[128,2,2048]{2,1,0:T(2,128)(2,1)}, u32[]{:S(2)}, u32[]{:S(2)}) async-start(bf16[128,2,2048]{2,1,0:T(2,128)(2,1)} %reshape.92), calls=%async_computation | async-start | bytes 2097152 | tf_op jit(solution)/shard_map/all_to_all | solution.py:171
  137.4 0.0 copy-done.2
  137.4 1.6 pad_maximum_fusion.w0_ref
  139.0 4.4 %collective-permute-start.2 = (bf16[3,192,2048]{2,1,0:T(8,128)(2,1)S(1)}, bf16[3,192,2048]{2,1,0:T(8,128)(2,1)}, u32[]{:S(2)}, u32[]{:S(2)}) collective-permute-start(bf16[3,192,2048]{2,1,0:T(8,128)(2,1)S(1)} %pad_maximum_fusion.w0_ref), channel_id=1, source_target_pairs={{0,24},{8,0},{16,8},{24,16},{1,25},{9,1},{17,9},{25,17},{2,26},{10... | collective-permute-start | bytes 7077896 | tf_op jit(solution)/shard_map/ppermute | solution.py:141
  143.4 2.3 collective-permute-start.1
  145.7 2.6 collective-permute-start
  148.3 40.7 %all-to-all-done = bf16[128,2,2048]{2,1,0:T(2,128)(2,1)} async-done(((bf16[128,2,2048]{2,1,0:T(2,128)(2,1)}), bf16[128,2,2048]{2,1,0:T(2,128)(2,1)}, u32[]{:S(2)}, u32[]{:S(2)}) %all-to-all-start) | async-done | bytes 1048608 | tf_op jit(solution)/shard_map/all_to_all | solution.py:171
  189.1 1.5 reshape.93.rows_ref
  190.6 3.2 collective-permute-done.2.w3_ref
  193.8 4.7 %collective-permute-done.1.w2_ref = bf16[3,192,2048]{2,1,0:T(8,128)(2,1)} collective-permute-done((bf16[3,192,2048]{2,1,0:T(8,128)(2,1)S(1)}, bf16[3,192,2048]{2,1,0:T(8,128)(2,1)}, u32[]{:S(2)}, u32[]{:S(2)}) %collective-permute-start.1) | collective-permute-done | bytes 2359328 | tf_op jit(solution)/shard_map/ppermute | solution.py:141
  198.5 52.1 %collective-permute-done.w1_ref = bf16[3,192,2048]{2,1,0:T(8,128)(2,1)} collective-permute-done((bf16[3,192,2048]{2,1,0:T(8,128)(2,1)S(1)}, bf16[3,192,2048]{2,1,0:T(8,128)(2,1)}, u32[]{:S(2)}, u32[]{:S(2)}) %collective-permute-start) | collective-permute-done | bytes 2359328 | tf_op jit(solution)/shard_map/ppermute | solution.py:141
  250.6 7.0 %shard_map.92 = bf16[256,2048]{1,0:T(8,128)(2,1)S(1)} custom-call(bf16[256,2048]{1,0:T(8,128)(2,1)S(1)} %reshape.93.rows_ref, bf16[3,192,2048]{2,1,0:T(8,128)(2,1)S(1)} %pad_maximum_fusion.w0_ref, bf16[3,192,2048]{2,1,0:T(8,128)(2,1)} %collective-permute-done.w1_ref, bf16[3,192,2048]{2,1,0:T(8,128)(2,1)} %collective-permute-done.1.w2_ref, ...), custom_call_target="tpu_custom_call" | custom-call | flops 2415919104 | bytes 11534336 | tf_op jit(solution)/shard_map/pallas_call | solution.py:97
  257.6 0.0 copy-start
  257.7 1.0 copy-done
  258.6 1.7 reshape.94
  260.4 0.0 copy-start.1
  260.4 0.0 copy-start.4
  260.4 68.2 %all_to_all.10 = bf16[128,2,2048]{2,1,0:T(2,128)(2,1)S(1)} all-to-all(bf16[128,2,2048]{2,1,0:T(2,128)(2,1)S(1)} %reshape.94), channel_id=1, replica_groups=mesh['z'=16,'yh'=2,'yl'=2,'e'=8] {'z','e'}, dimensions={0} | all-to-all | bytes 2097152 | tf_op jit(solution)/shard_map/all_to_all | solution.py:176
  328.6 0.4 reshape.95
  329.0 0.0 copy-done.1
  329.0 0.0 copy-done.4
  329.0 1.2 fusion.2
  (1 shorter events, 0.0 us)
Async XLA Ops:
  6.5 83.2 %all-gather.4.cloned.1.call-start = ((), (), s32[]{:S(2)}) async-start(), calls=%async_computation.2 | async-start | bytes 4456448 | tf_op jit(solution)/shard_map/all_gather | solution.py:134
  89.7 23.6 %copy-start.3 = (f32[2048]{0:T(1024)S(1)}, f32[2048]{0:T(1024)}, u32[]{:S(2)}) copy-start(f32[2048]{0:T(1024)} %param.13) | copy-start | bytes 24580
  114.9 22.5 %copy-start.2 = (bf16[1,1,192,2048]{3,2,1,0:T(8,128)(2,1)S(1)}, bf16[1,1,192,2048]{3,2,1,0:T(8,128)(2,1)}, u32[]{:S(2)}) copy-start(bf16[1,1,192,2048]{3,2,1,0:T(8,128)(2,1)} %param.17) | copy-start | bytes 2359300
  116.4 72.6 %all-to-all-start = ((bf16[128,2,2048]{2,1,0:T(2,128)(2,1)}), bf16[128,2,2048]{2,1,0:T(2,128)(2,1)}, u32[]{:S(2)}, u32[]{:S(2)}) async-start(bf16[128,2,2048]{2,1,0:T(2,128)(2,1)} %reshape.92), calls=%async_computation | async-start | bytes 2097152 | tf_op jit(solution)/shard_map/all_to_all | solution.py:171
  139.0 54.8 %collective-permute-start.2 = (bf16[3,192,2048]{2,1,0:T(8,128)(2,1)S(1)}, bf16[3,192,2048]{2,1,0:T(8,128)(2,1)}, u32[]{:S(2)}, u32[]{:S(2)}) collective-permute-start(bf16[3,192,2048]{2,1,0:T(8,128)(2,1)S(1)} %pad_maximum_fusion.w0_ref), channel_id=1, source_target_pairs={{0,24},{8,0},{16,8},{24,16},{1,25},{9,1},{17,9},{25,17},{2,26},{10... | collective-permute-start | bytes 7077896 | tf_op jit(solution)/shard_map/ppermute | solution.py:141
  143.4 55.1 %collective-permute-start.1 = (bf16[3,192,2048]{2,1,0:T(8,128)(2,1)S(1)}, bf16[3,192,2048]{2,1,0:T(8,128)(2,1)}, u32[]{:S(2)}, u32[]{:S(2)}) collective-permute-start(bf16[3,192,2048]{2,1,0:T(8,128)(2,1)S(1)} %pad_maximum_fusion.w0_ref), channel_id=1, source_target_pairs={{0,16},{8,24},{16,0},{24,8},{1,17},{9,25},{17,1},{25,9},{2,18},{10... | collective-permute-start | bytes 7077896 | tf_op jit(solution)/shard_map/ppermute | solution.py:141
  145.7 104.9 %collective-permute-start = (bf16[3,192,2048]{2,1,0:T(8,128)(2,1)S(1)}, bf16[3,192,2048]{2,1,0:T(8,128)(2,1)}, u32[]{:S(2)}, u32[]{:S(2)}) collective-permute-start(bf16[3,192,2048]{2,1,0:T(8,128)(2,1)S(1)} %pad_maximum_fusion.w0_ref), channel_id=1, source_target_pairs={{0,8},{8,16},{16,24},{24,0},{1,9},{9,17},{17,25},{25,1},{2,10},{10... | collective-permute-start | bytes 7077896 | tf_op jit(solution)/shard_map/ppermute | solution.py:141
  257.6 1.0 copy-start
  260.4 68.7 %copy-start.1 = (bf16[128,2048]{1,0:T(8,128)(2,1)S(1)}, bf16[128,2048]{1,0:T(8,128)(2,1)}, u32[]{:S(2)}) copy-start(bf16[128,2048]{1,0:T(8,128)(2,1)} %shard_map.91) | copy-start | bytes 1572868
  260.4 68.7 %copy-start.4 = (f32[1,128,1]{1,2,0:T(1,128)S(1)}, f32[1,128,1]{1,2,0:T(1,128)}, u32[]{:S(2)}) copy-start(f32[1,128,1]{1,2,0:T(1,128)} %param.15) | copy-start | bytes 1540
Sparse Core Ops, SparseCore 0:
  14.4 75.2 all-gather.3
